TPU v7x, 768 devices: a whole 4x8x12 slice. The times are simulated.
768 devices in a mesh: shard: 16 (over x_hi, y), rep: 48 (over x_lo, z, core).
Axes of the slice: x: 4 (x_hi: 2, x_lo: 2; x = x_hi * 2 + x_lo), y: 8, z: 12, core: 2. Of those that a mesh axis runs over, the one named last changes fastest.
Arguments:
- hidden_act: bfloat16 [1536, 196, 3072], P(('shard', 'rep')), may hold values from -24 to 24
- out_grad: bfloat16 [1536, 196, 768], P(('shard', 'rep')), may hold values from -0.23925781 to 0.23925781
- grn_gamma: float32 [3072], replicated, may hold values from -4 to 4
- grn_beta: float32 [3072], replicated, may hold values from -4 to 4
- master: float32 [3072, 768], P('shard'), may hold values from -0.109375 to 0.109375
- moment_one: float32 [3072, 768], P('shard'), may hold values from -5 to 5
- moment_two: float32 [3072, 768], P('shard'), may hold values from 0.1 to 2
Outputs:
- new_master: float32 [3072, 768], P('shard')
- new_moment_one: float32 [3072, 768], P('shard')
- new_moment_two: float32 [3072, 768], P('shard')
- weights: bfloat16 [3072, 768], P(None, 'rep')
All inputs are finite; a program needn't handle non-finite values.
Results may differ from a plain program's by a relative error of at most 0.02.
Values may be sent and summed in bfloat16 or wider, within the bound.
No kernel may reach another device: no remote copies, remote signals or barrier semaphores. Data moves between devices by JAX's collectives and lax.ppermute only.
A program may use at most 64 MiB of HBM per device.

v0:
```python
import jax
import jax.numpy as jnp
from jax import lax
from jax.sharding import PartitionSpec as P

learn_rate = 0.001
beta_one = 0.9
beta_two = 0.999
adam_eps = 1e-08
decay_rate = 0.05
step_count = 10


def grn_forward(images, grn_gamma, grn_beta):
    values = images.astype(jnp.float32)
    spatial_norm = jnp.sqrt(jnp.sum(values * values, axis=1))
    ratio = spatial_norm / (jnp.mean(spatial_norm, axis=1, keepdims=True) + 1e-06)
    grn_out = grn_gamma * (values * ratio[:, None, :]) + grn_beta + values
    return grn_out.astype(jnp.bfloat16)


def body(hidden_act, out_grad, grn_gamma, grn_beta, master, moment_one, moment_two):
    images, positions, hidden = hidden_act.shape
    channels = out_grad.shape[2]
    flat_rows = grn_forward(hidden_act, grn_gamma, grn_beta).reshape(images * positions, hidden)
    flat_grads = out_grad.reshape(images * positions, channels)
    term = lax.dot_general(
        flat_rows, flat_grads, (((0,), (0,)), ((), ())), preferred_element_type=jnp.float32
    )
    rounded = lax.optimization_barrier(term.astype(jnp.bfloat16))
    group_sum = lax.psum_scatter(
        rounded.astype(jnp.float32).astype(jnp.bfloat16), "shard", scatter_dimension=0, tiled=True
    ).astype(jnp.float32)
    grad = lax.psum(group_sum, "rep")
    new_moment_one = beta_one * moment_one + (1.0 - beta_one) * grad
    new_moment_two = beta_two * moment_two + (1.0 - beta_two) * grad * grad
    corrected_one = new_moment_one / (1.0 - beta_one**step_count)
    corrected_two = new_moment_two / (1.0 - beta_two**step_count)
    update = corrected_one / (jnp.sqrt(corrected_two) + adam_eps) + decay_rate * master
    new_master = master - learn_rate * update
    own_width = channels // lax.axis_size("rep")
    own_start = lax.axis_index("rep") * own_width
    own_columns = lax.dynamic_slice_in_dim(new_master.astype(jnp.bfloat16), own_start, own_width, 1)
    weights = lax.all_gather(own_columns, "shard", axis=0, tiled=True)
    return (new_master, new_moment_one, new_moment_two, weights)


def solution(mesh):
    in_specs = (
        P(("shard", "rep"), None, None),
        P(("shard", "rep"), None, None),
        P(),
        P(),
        P("shard", None),
        P("shard", None),
        P("shard", None),
    )
    out_specs = (P("shard", None), P("shard", None), P("shard", None), P(None, "rep"))
    return jax.shard_map(body, mesh=mesh, in_specs=in_specs, out_specs=out_specs, check_vma=False)
```

profile of v0, /device:TPU:6, one launch (start us, length us, event | category | flops | bytes accessed | tf_op | source)
XLA Modules:
  0.0 465.5 jit_solution(12045337064924024426)
XLA Ops:
  7.2 0.0 copy-start
  7.2 0.0 reduce-scatter.2.cloned.1.call-start
  7.2 4.3 fusion
  11.5 0.1 sqrt_reduce_fusion
  11.7 0.1 sqrt_divide_fusion
  11.7 5.4 %fusion.3 = bf16[2,196,3072]{2,0,1:T(2,128)(2,1)S(1)} fusion(bf16[2,196,3072]{2,0,1:T(2,128)(2,1)} %param.7, f32[3072]{0:T(1024)} %param.10, f32[2,3072]{1,0:T(2,128)S(1)} %sqrt_divide_fusion, f32[3072]{0:T(1024)} %param.9), kind=kLoop, calls=%fused_computation.7 | loop fusion | flops 7225344 | bytes 4866048 | tf_op jit(solution)/shard_map/convert_element_type | solution.py:19
  17.2 0.0 copy-done
  17.2 4.4 bitcast_convert_fusion
  21.5 0.0 copy-start.2
  21.6 0.0 copy-start.3
  21.6 0.0 copy-start.4
  21.6 0.0 reduce-scatter.2.cloned.1.call-update
  21.6 232.4 %reduce-scatter.2.cloned.1.call-done = bf16[192,768]{1,0:T(8,128)(2,1)} async-done(((bf16[3072,768]{1,0:T(8,128)(2,1)}), bf16[192,768]{1,0:T(8,128)(2,1)}) %reduce-scatter.2.cloned.1.call-update) | async-done | bytes 294928 | tf_op jit(solution)/shard_map/reduce_scatter | solution.py:31
  254.0 161.4 %all-reduce.1 = f32[192,768]{1,0:T(8,128)S(1)} all-reduce(bf16[192,768]{1,0:T(8,128)(2,1)} %reduce-scatter.2.cloned.1.call-done), channel_id=1, replica_groups=mesh['shard'=16,'rep'=48] {'rep'}, use_global_device_ids=true, to_apply=%region_3.0 | all-reduce | flops 147456 | bytes 884736 | tf_op jit(solution)/shard_map/psum | solution.py:34
  415.4 0.0 copy-done.2
  415.4 0.0 copy-done.3
  415.4 0.0 copy-done.4
  415.4 1.4 multiply_subtract_fusion
  416.9 0.0 copy-start.1
  416.9 0.1 dynamic-slice_convert_fusion
  417.0 0.1 copy.22
  417.0 40.8 %all-gather = bf16[16,192,16]{1,2,0:T(8,128)(2,1)S(1)} all-gather(bf16[1,192,16]{1,2,0:T(8,128)(2,1)S(1)} %bitcast.5), channel_id=1, replica_groups=mesh['shard'=16,'rep'=48] {'shard'}, dimensions={0}, use_global_device_ids=true | all-gather | bytes 104448 | tf_op jit(solution)/shard_map/all_gather | solution.py:44
  457.9 0.8 reshape.34
  458.7 0.0 copy-done.1
  (2 shorter events, 0.0 us)
Async XLA Ops:
  7.2 10.0 %copy-start = (bf16[2,196,768]{2,0,1:T(2,128)(2,1)S(1)}, bf16[2,196,768]{2,0,1:T(2,128)(2,1)}, u32[]{:S(2)}) copy-start(bf16[2,196,768]{2,0,1:T(2,128)(2,1)} %param.8) | copy-start | bytes 1806340
  7.2 246.8 %reduce-scatter.2.cloned.1.call-start = ((), (), s32[]{:S(2)}) async-start(), calls=%async_computation.1 | async-start | bytes 5013504 | tf_op jit(solution)/shard_map/reduce_scatter | solution.py:31
  21.5 393.9 %copy-start.2 = (f32[192,768]{1,0:T(8,128)S(1)}, f32[192,768]{1,0:T(8,128)}, u32[]{:S(2)}) copy-start(f32[192,768]{1,0:T(8,128)} %param.11) | copy-start | bytes 1769476
  21.6 393.9 %copy-start.3 = (f32[192,768]{1,0:T(8,128)S(1)}, f32[192,768]{1,0:T(8,128)}, u32[]{:S(2)}) copy-start(f32[192,768]{1,0:T(8,128)} %param.12) | copy-start | bytes 1769476
  21.6 393.9 %copy-start.4 = (f32[192,768]{1,0:T(8,128)S(1)}, f32[192,768]{1,0:T(8,128)}, u32[]{:S(2)}) copy-start(f32[192,768]{1,0:T(8,128)} %param.13) | copy-start | bytes 1769476
  416.9 41.8 %copy-start.1 = (f32[192,768]{1,0:T(8,128)}, f32[192,768]{1,0:T(8,128)S(1)}, u32[]{:S(2)}) copy-start(f32[192,768]{1,0:T(8,128)S(1)} %get-tuple-element.4) | copy-start | bytes 1769476
Sparse Core Ops, SparseCore 0:
  21.7 232.2 reduce-scatter.1
where the time goes:
time: 466 us
  waiting for transfers between devices  232 us (50%)
  blocking collectives  202 us (43%)
  between operations  14.1 us (3%)
  other arithmetic  11.4 us (2%)
    reduce_scatter x1, waiting for transfers between devices, body(): lax.psum_scatter(rounded.astype(jnp.float32).astype(jnp.bfloat16), 'shard...  232 us
    psum x1, blocking collectives, body(): grad = lax.psum(group_sum, 'rep')  161 us
    all_gather x1, blocking collectives, body(): weights = lax.all_gather(own_columns, 'shard', axis=0, tiled=True)  40.8 us
  transfers between devices with their start and end apart: 1, of which 1 were waited for; matrix products, arithmetic and copies ran while one was open for 0% of the time, Pallas kernels for 0%

commit v1 on v0

v1 whole, which is shorter than its diff:
```python
import jax
import jax.numpy as jnp
import numpy as np
from jax import lax
from jax.sharding import Mesh
from jax.sharding import PartitionSpec as P

learn_rate = 0.001
beta_one = 0.9
beta_two = 0.999
adam_eps = 1e-08
decay_rate = 0.05
step_count = 10
CORES = 2
SWAP = [(0, 1), (1, 0)]


def grn_forward(images, grn_gamma, grn_beta):
    values = images.astype(jnp.float32)
    spatial_norm = jnp.sqrt(jnp.sum(values * values, axis=1))
    ratio = spatial_norm / (jnp.mean(spatial_norm, axis=1, keepdims=True) + 1e-06)
    grn_out = grn_gamma * (values * ratio[:, None, :]) + grn_beta + values
    return grn_out.astype(jnp.bfloat16)


def by_core(core, mine, other):
    return jnp.where(core == 0, jnp.concatenate([mine, other], 1), jnp.concatenate([other, mine], 1))


def body(hidden_act, out_grad, grn_gamma, grn_beta, master, moment_one, moment_two):
    images, positions, hidden = hidden_act.shape
    channels = out_grad.shape[2]
    flat_rows = grn_forward(hidden_act, grn_gamma, grn_beta).reshape(images * positions, hidden)
    flat_grads = out_grad.reshape(images * positions, channels)
    term = lax.dot_general(
        flat_rows, flat_grads, (((0,), (0,)), ((), ())), preferred_element_type=jnp.float32
    ).astype(jnp.bfloat16)
    core = lax.axis_index("c")
    half = channels // CORES
    mine = lax.dynamic_slice_in_dim(term, core * half, half, 1)
    other = lax.dynamic_slice_in_dim(term, (1 - core) * half, half, 1)
    chip = mine.astype(jnp.float32) + lax.ppermute(other, "c", SWAP).astype(jnp.float32)
    n_shard = lax.axis_size("shard")
    block = hidden // n_shard
    pieces = lax.all_to_all(
        chip.astype(jnp.bfloat16).reshape(n_shard, block, half), "shard", 0, 0, tiled=True
    )
    part = jnp.sum(pieces.astype(jnp.float32), axis=0)
    n_rq = lax.axis_size("rq")
    sub = block // n_rq
    pieces2 = lax.all_to_all(part.reshape(n_rq, sub, half), "rq", 0, 0, tiled=True)
    grad_sub = jnp.sum(pieces2, axis=0)
    grad_half = lax.all_gather(grad_sub, "rq", axis=0, tiled=True)
    grad = by_core(core, grad_half, lax.ppermute(grad_half, "c", SWAP))
    new_moment_one = beta_one * moment_one + (1.0 - beta_one) * grad
    new_moment_two = beta_two * moment_two + (1.0 - beta_two) * grad * grad
    corrected_one = new_moment_one / (1.0 - beta_one**step_count)
    corrected_two = new_moment_two / (1.0 - beta_two**step_count)
    update = corrected_one / (jnp.sqrt(corrected_two) + adam_eps) + decay_rate * master
    new_master = master - learn_rate * update
    n_rep = n_rq * CORES
    own_width = channels // n_rep
    own_start = (lax.axis_index("rq") * CORES + core) * own_width
    own_columns = lax.dynamic_slice_in_dim(new_master.astype(jnp.bfloat16), own_start, own_width, 1)
    weights = lax.all_gather(own_columns, "shard", axis=0, tiled=True)
    return (new_master, new_moment_one, new_moment_two, weights)


def solution(mesh):
    n_shard, n_rep = mesh.shape["shard"], mesh.shape["rep"]
    devices = np.asarray(mesh.devices).reshape(n_shard, n_rep // CORES, CORES)
    fine = Mesh(devices, ("shard", "rq", "c"))
    rows = ("shard", "rq", "c")
    in_specs = (
        P(rows, None, None),
        P(rows, None, None),
        P(),
        P(),
        P("shard", None),
        P("shard", None),
        P("shard", None),
    )
    out_specs = (P("shard", None), P("shard", None), P("shard", None), P(None, ("rq", "c")))
    return jax.shard_map(body, mesh=fine, in_specs=in_specs, out_specs=out_specs, check_vma=False)
```

time: 466 us -> 226 us (0.48)
  waiting for transfers between devices: 232 us -> 4.71 us
  blocking collectives: 202 us -> 183 us
  between operations: 14.1 us -> 0.77 us
  local copies, waits for them, and re-layouts: 1.02 us -> 14.1 us
    reduce_scatter x1 -> x0, waiting for transfers between devices: 232 us -> none  [body(): lax.psum_scatter(rounded.astype(jnp.float32).astype(jnp.bfloat16), 'shard...]
    psum x1 -> x0, blocking collectives: 161 us -> none  [body(): grad = lax.psum(group_sum, 'rep')]
    all_to_all x0 -> x2, blocking collectives: none -> 94.4 us  [the longest x1 64.7 us: body(): lax.all_to_all(chip.astype(jnp.bfloat16).reshape(n_shard, block, half), '...]
    all_gather x0 -> x1, blocking collectives: none -> 47.6 us  [body(): grad_half = lax.all_gather(grad_sub, 'rq', axis=0, tiled=True)]
    unnamed x11 -> x14, local copies, waits for them, and re-layouts: 0.83 us -> 12.2 us
    ppermute x0 -> x2, waiting for transfers between devices: none -> 4.71 us  [the longest x1 4.71 us: body(): lax.ppermute(other, 'c', SWAP).astype(jnp.float32)]
  transfers between devices with their start and end apart: 1 -> 2, of which waited for: 1 -> 1; matrix products, arithmetic and copies ran while one was open for 0% -> 2% of each run, Pallas kernels for 0% -> 0%
where the time goes in v1:
time: 226 us
  blocking collectives  183 us (81%)
  other arithmetic  15.9 us (7%)
  local copies, waits for them, and re-layouts  14.1 us (6%)
  waiting for transfers between devices  4.71 us (2%)
  starting transfers between devices  3.83 us (2%)
  matrix products  3 us (1%)
    all_to_all x1, blocking collectives, body(): lax.all_to_all(chip.astype(jnp.bfloat16).reshape(n_shard, block, half), '...  64.7 us
    all_gather x1, blocking collectives, body(): grad_half = lax.all_gather(grad_sub, 'rq', axis=0, tiled=True)  47.6 us
    all_gather x1, blocking collectives, body(): weights = lax.all_gather(own_columns, 'shard', axis=0, tiled=True)  41.3 us
    all_to_all x1, blocking collectives, body(): lax.all_to_all(part.reshape(n_rq, sub, half), 'rq', 0, 0, tiled=True)  29.7 us
    unnamed x14, local copies, waits for them, and re-layouts  12.2 us
    convert_element_type x1, other arithmetic, grn_forward(): return grn_out.astype(jnp.bfloat16)  5.42 us
    ppermute x1, waiting for transfers between devices, body(): lax.ppermute(other, 'c', SWAP).astype(jnp.float32)  4.71 us
  transfers between devices with their start and end apart: 2, of which 1 were waited for; matrix products, arithmetic and copies ran while one was open for 2% of the time, Pallas kernels for 0%

profile of v1, /device:TPU:6, one launch (start us, length us, event | category | flops | bytes accessed | tf_op | source)
XLA Modules:
  0.0 225.7 jit_solution(17430192210227754055)
XLA Ops:
  0.6 0.0 copy-start
  0.7 4.3 %fusion = f32[2,3072]{1,0:T(2,128)S(1)} fusion(bf16[2,196,3072]{2,0,1:T(2,128)(2,1)} %param.7), kind=kLoop, calls=%fused_computation.4 | loop fusion | flops 3606528 | bytes 2433024 | tf_op jit(solution)/shard_map/reduce_sum | solution.py:20
  4.9 0.1 sqrt_reduce_fusion
  5.1 0.1 sqrt_divide_fusion
  5.2 5.4 %fusion.3 = bf16[2,196,3072]{2,0,1:T(2,128)(2,1)S(1)} fusion(bf16[2,196,3072]{2,0,1:T(2,128)(2,1)} %param.7, f32[3072]{0:T(1024)} %param.10, f32[2,3072]{1,0:T(2,128)S(1)} %sqrt_divide_fusion, f32[3072]{0:T(1024)} %param.9), kind=kLoop, calls=%fused_computation.7 | loop fusion | flops 7225344 | bytes 4866048 | tf_op jit(solution)/shard_map/convert_element_type | solution.py:23
  10.6 0.0 copy-done
  10.6 3.0 %bitcast_convert_fusion = bf16[3072,768]{1,0:T(8,128)(2,1)S(1)} fusion(bf16[2,196,3072]{2,0,1:T(2,128)(2,1)S(1)} %fusion.3, bf16[2,196,768]{2,0,1:T(2,128)(2,1)S(1)} %copy-done), kind=kOutput, calls=%fused_computation | convolution fusion | flops 1852047360 | bytes 7729152 | tf_op jit(solution)/shard_map/dot_general | solution.py:35
  13.6 0.0 copy-start.1
  13.6 2.1 copy-done.1
  15.7 1.7 constant_dynamic-slice_fusion
  17.4 1.9 collective-permute-start
  19.3 4.7 %collective-permute-done = bf16[3072,384]{1,0:T(8,128)(2,1)S(1)} collective-permute-done((bf16[3072,384]{1,0:T(8,128)(2,1)}, bf16[3072,384]{1,0:T(8,128)(2,1)S(1)}, u32[]{:S(2)}, u32[]{:S(2)}) %collective-permute-start) | collective-permute-done | bytes 2359328 | tf_op jit(solution)/shard_map/ppermute | solution.py:42
  24.1 2.3 %add_convert_fusion = bf16[3072,384]{1,0:T(8,128)(2,1)S(1)} fusion(bf16[3072,384]{1,0:T(8,128)(2,1)S(1)} %collective-permute-done, bf16[3072,768]{1,0:T(8,128)(2,1)} %copy-done.1, s32[]{:T(128)S(6)} %select_n.18), kind=kLoop, calls=%fused_computation.9 | loop fusion | flops 4718592 | bytes 7077892 | tf_op jit(solution)/shard_map/convert_element_type | solution.py:46
  26.4 0.0 copy-start.2
  26.4 64.7 %all_to_all.10 = bf16[16,192,384]{2,1,0:T(8,128)(2,1)S(1)} all-to-all(bf16[16,192,384]{2,1,0:T(8,128)(2,1)S(1)} %bitcast.8), channel_id=1, replica_groups=mesh['shard'=16,'rq'=24,'c'=2] {'shard'}, dimensions={0} | all-to-all | bytes 4718592 | tf_op jit(solution)/shard_map/all_to_all | solution.py:45
  91.1 0.3 convert_reduce_fusion
  91.4 29.7 %all_to_all.11 = f32[24,8,384]{2,1,0:T(8,128)S(1)} all-to-all(f32[24,8,384]{2,1,0:T(8,128)S(1)} %bitcast.9), channel_id=1, replica_groups=mesh['shard'=16,'rq'=24,'c'=2] {'rq'}, dimensions={0} | all-to-all | bytes 589824 | tf_op jit(solution)/shard_map/all_to_all | solution.py:51
  121.2 47.6 %all_gather.6 = f32[192,384]{1,0:T(8,128)S(1)} all-gather(f32[8,384]{1,0:T(8,128)S(1)} %reduce_sum.39), channel_id=1, replica_groups=mesh['shard'=16,'rq'=24,'c'=2] {'rq'}, dimensions={0}, use_global_device_ids=true | all-gather | bytes 307200 | tf_op jit(solution)/shard_map/all_gather | solution.py:53
  168.8 0.2 copy.49
  169.0 1.9 collective-permute-start.1
  170.9 0.0 copy-done.2
  170.9 0.3 copy.45
  171.2 1.3 copy.51
  172.5 2.2 copy.53
  174.8 0.0 collective-permute-done.1
  174.8 3.2 %multiply_subtract_fusion = (f32[192,768]{0,1:T(8,128)S(1)}, f32[192,768]{0,1:T(8,128)}, f32[192,768]{0,1:T(8,128)}) fusion(f32[192,768]{0,1:T(8,128)} %copy.53, f32[192,384]{0,1:T(8,128)S(1)} %copy.49, f32[192,384]{0,1:T(8,128)} %collective-permute-done.1, pred[]{:T(512)S(6)} %eq.3, f32[192,768]{0,1:T(8,128)S(1)} %copy.45, f32[192,768]{0,1:T(8,128)S(1)} %copy.51), kind=kLoop, calls=%fused_computation.14 | loop fusion | flops 2654208 | bytes 4128769 | tf_op jit(solution)/shard_map/sub | solution.py:60
  178.0 1.1 copy.55
  179.1 2.2 copy.56
  181.3 2.2 copy.57
  183.5 41.3 %all-gather = bf16[16,192,16]{1,2,0:T(8,128)(2,1)S(1)} all-gather(bf16[1,192,16]{1,2,0:T(8,128)(2,1)S(1)} %fusion.7), channel_id=1, replica_groups=mesh['shard'=16,'rq'=24,'c'=2] {'shard'}, dimensions={0}, use_global_device_ids=true | all-gather | bytes 104448 | tf_op jit(solution)/shard_map/all_gather | solution.py:65
  224.8 0.8 reshape.42
  (4 shorter events, 0.1 us)
Async XLA Ops:
  0.6 10.0 %copy-start = (bf16[2,196,768]{2,0,1:T(2,128)(2,1)S(1)}, bf16[2,196,768]{2,0,1:T(2,128)(2,1)}, u32[]{:S(2)}) copy-start(bf16[2,196,768]{2,0,1:T(2,128)(2,1)} %param.8) | copy-start | bytes 1806340
  13.6 2.1 copy-start.1
  17.4 6.6 %collective-permute-start = (bf16[3072,384]{1,0:T(8,128)(2,1)}, bf16[3072,384]{1,0:T(8,128)(2,1)S(1)}, u32[]{:S(2)}, u32[]{:S(2)}) collective-permute-start(bf16[3072,384]{1,0:T(8,128)(2,1)} %constant_dynamic-slice_fusion), channel_id=1, source_target_pairs={{0,1},{1,0},{2,3},{3,2},{4,5},{5,4},{6,7},{7,6},{8,9},{9,8},{10,11... | collective-permute-start | bytes 7077896 | tf_op jit(solution)/shard_map/ppermute | solution.py:42
  26.4 144.5 %copy-start.2 = (f32[192,768]{1,0:T(8,128)S(1)}, f32[192,768]{1,0:T(8,128)}, u32[]{:S(2)}) copy-start(f32[192,768]{1,0:T(8,128)} %param.12) | copy-start | bytes 1769476
  169.0 5.8 %collective-permute-start.1 = (f32[192,384]{0,1:T(8,128)S(1)}, f32[192,384]{0,1:T(8,128)}, u32[]{:S(2)}, u32[]{:S(2)}) collective-permute-start(f32[192,384]{0,1:T(8,128)S(1)} %copy.49), channel_id=1, source_target_pairs={{0,1},{1,0},{2,3},{3,2},{4,5},{5,4},{6,7},{7,6},{8,9},{9,8},{10,11... | collective-permute-start | bytes 884744 | tf_op jit(solution)/shard_map/ppermute | solution.py:54

commit v2 on v1

--- a/solution.py
+++ b/solution.py
@@ -46,31 +46,44 @@
         chip.astype(jnp.bfloat16).reshape(n_shard, block, half), "shard", 0, 0, tiled=True
     )
     part = jnp.sum(pieces.astype(jnp.float32), axis=0)
-    n_rq = lax.axis_size("rq")
-    sub = block // n_rq
-    pieces2 = lax.all_to_all(part.reshape(n_rq, sub, half), "rq", 0, 0, tiled=True)
+    x_lo = lax.axis_index("xl")
+    rows_half = block // 2
+    mine_rows = lax.dynamic_slice_in_dim(part, x_lo * rows_half, rows_half, 0)
+    other_rows = lax.dynamic_slice_in_dim(part, (1 - x_lo) * rows_half, rows_half, 0)
+    part_half = mine_rows + lax.ppermute(other_rows, "xl", SWAP)
+    n_z = lax.axis_size("z")
+    sub = rows_half // n_z
+    pieces2 = lax.all_to_all(part_half.reshape(n_z, sub, half), "z", 0, 0, tiled=True)
     grad_sub = jnp.sum(pieces2, axis=0)
-    grad_half = lax.all_gather(grad_sub, "rq", axis=0, tiled=True)
-    grad = by_core(core, grad_half, lax.ppermute(grad_half, "c", SWAP))
+    spread = jnp.broadcast_to(grad_sub[None], (n_z, sub, half))
+    grad_quarter = lax.all_to_all(spread, "z", 0, 0, tiled=True).reshape(rows_half, half)
+    from_x = lax.ppermute(grad_quarter, "xl", SWAP)
+    from_core = lax.ppermute(grad_quarter, "c", SWAP)
+    from_both = lax.ppermute(grad_quarter, ("xl", "c"), [(0, 3), (3, 0), (1, 2), (2, 1)])
+    own_half = by_core(core, grad_quarter, from_core)
+    far_half = by_core(core, from_x, from_both)
+    grad = jnp.where(x_lo == 0, jnp.concatenate([own_half, far_half], 0), jnp.concatenate([far_half, own_half], 0))
     new_moment_one = beta_one * moment_one + (1.0 - beta_one) * grad
     new_moment_two = beta_two * moment_two + (1.0 - beta_two) * grad * grad
     corrected_one = new_moment_one / (1.0 - beta_one**step_count)
     corrected_two = new_moment_two / (1.0 - beta_two**step_count)
     update = corrected_one / (jnp.sqrt(corrected_two) + adam_eps) + decay_rate * master
     new_master = master - learn_rate * update
-    n_rep = n_rq * CORES
+    n_rep = lax.axis_size(("xl", "z", "c"))
     own_width = channels // n_rep
-    own_start = (lax.axis_index("rq") * CORES + core) * own_width
+    own_start = lax.axis_index(("xl", "z", "c")) * own_width
     own_columns = lax.dynamic_slice_in_dim(new_master.astype(jnp.bfloat16), own_start, own_width, 1)
-    weights = lax.all_gather(own_columns, "shard", axis=0, tiled=True)
+    spread_cols = jnp.broadcast_to(own_columns[None], (n_shard, block, own_width))
+    weights = lax.all_to_all(spread_cols, "shard", 0, 0, tiled=True).reshape(hidden, own_width)
     return (new_master, new_moment_one, new_moment_two, weights)
 
 
 def solution(mesh):
     n_shard, n_rep = mesh.shape["shard"], mesh.shape["rep"]
-    devices = np.asarray(mesh.devices).reshape(n_shard, n_rep // CORES, CORES)
-    fine = Mesh(devices, ("shard", "rq", "c"))
-    rows = ("shard", "rq", "c")
+    x_lo = 2
+    devices = np.asarray(mesh.devices).reshape(n_shard, x_lo, n_rep // (x_lo * CORES), CORES)
+    fine = Mesh(devices, ("shard", "xl", "z", "c"))
+    rows = ("shard", "xl", "z", "c")
     in_specs = (
         P(rows, None, None),
         P(rows, None, None),
@@ -80,5 +93,5 @@
         P("shard", None),
         P("shard", None),
     )
-    out_specs = (P("shard", None), P("shard", None), P("shard", None), P(None, ("rq", "c")))
+    out_specs = (P("shard", None), P("shard", None), P("shard", None), P(None, ("xl", "z", "c")))
     return jax.shard_map(body, mesh=fine, in_specs=in_specs, out_specs=out_specs, check_vma=False)

time: 226 us -> 178 us (0.79)
  blocking collectives: 183 us -> 57.8 us
  waiting for transfers between devices: 4.71 us -> 67.3 us
  starting transfers between devices: 3.83 us -> 24.7 us
  local copies, waits for them, and re-layouts: 14.1 us -> 4.86 us
    all_gather x2 -> x0, blocking collectives: 88.9 us -> none  [the longest x1 47.6 us: body(): grad_half = lax.all_gather(grad_sub, 'rq', axis=0, tiled=True)]
    all_to_all x0 -> x1, waiting for transfers between devices: none -> 54.4 us  [body(): lax.all_to_all(chip.astype(jnp.bfloat16).reshape(n_shard, block, half), '...]
    all_to_all x2 -> x3, blocking collectives: 94.4 us -> 57.8 us  [the longest x1 25.3 us: body(): lax.all_to_all(part_half.reshape(n_z, sub, half), 'z', 0, 0, tiled=True)]
    ppermute x1 -> x4, starting transfers between devices: 1.92 us -> 12.7 us  [the longest x1 5.15 us: body(): part_half = mine_rows + lax.ppermute(other_rows, 'xl', SWAP)]
    unnamed x14 -> x6, local copies, waits for them, and re-layouts: 12.2 us -> 2.13 us
    all_to_all x0 -> x1, starting transfers between devices: none -> 10.1 us  [body(): lax.all_to_all(chip.astype(jnp.bfloat16).reshape(n_shard, block, half), '...]
    ppermute x1 -> x4, waiting for transfers between devices: 0.01 us -> 8.18 us  [the longest x1 3.1 us: body(): part_half = mine_rows + lax.ppermute(other_rows, 'xl', SWAP)]
  transfers between devices with their start and end apart: 2 -> 6, of which waited for: 1 -> 5; matrix products, arithmetic and copies ran while one was open for 2% -> 0% of each run, Pallas kernels for 0% -> 0%
where the time goes in v2:
time: 178 us; the launch traced here: 176 us
  waiting for transfers between devices  67.3 us (38%)
  blocking collectives  57.8 us (32%)
  starting transfers between devices  24.7 us (14%)
  other arithmetic  17 us (10%)
  local copies, waits for them, and re-layouts  4.86 us (3%)
  matrix products  3 us (2%)
    all_to_all x1, waiting for transfers between devices, body(): lax.all_to_all(chip.astype(jnp.bfloat16).reshape(n_shard, block, half), '...  54.4 us
    all_to_all x1, blocking collectives, body(): lax.all_to_all(part_half.reshape(n_z, sub, half), 'z', 0, 0, tiled=True)  25.3 us
    all_to_all x1, blocking collectives, body(): lax.all_to_all(spread_cols, 'shard', 0, 0, tiled=True)  17.7 us
    all_to_all x1, blocking collectives, body(): lax.all_to_all(spread, 'z', 0, 0, tiled=True).reshape(rows_half, half)  14.8 us
    all_to_all x1, starting transfers between devices, body(): lax.all_to_all(chip.astype(jnp.bfloat16).reshape(n_shard, block, half), '...  10.1 us
    convert_element_type x1, other arithmetic, grn_forward(): return grn_out.astype(jnp.bfloat16)  5.42 us
    ppermute x1, starting transfers between devices, body(): part_half = mine_rows + lax.ppermute(other_rows, 'xl', SWAP)  5.15 us
    ppermute x1, waiting for transfers between devices, body(): lax.ppermute(other, 'c', SWAP).astype(jnp.float32)  4.71 us
  transfers between devices with their start and end apart: 6, of which 5 were waited for; matrix products, arithmetic and copies ran while one was open for 0% of the time, Pallas kernels for 0%

profile of v2, /device:TPU:6, one launch (start us, length us, event | category | flops | bytes accessed | tf_op | source)
XLA Modules:
  0.0 175.5 jit_solution(17772251382651355634)
XLA Ops:
  0.6 0.0 copy-start
  0.7 4.3 %fusion = f32[2,3072]{1,0:T(2,128)S(1)} fusion(bf16[2,196,3072]{2,0,1:T(2,128)(2,1)} %param.7), kind=kLoop, calls=%fused_computation.4 | loop fusion | flops 3606528 | bytes 2433024 | tf_op jit(solution)/shard_map/reduce_sum | solution.py:20
  4.9 0.1 sqrt_reduce_fusion
  5.1 0.1 sqrt_divide_fusion
  5.2 5.4 %fusion.3 = bf16[2,196,3072]{2,0,1:T(2,128)(2,1)S(1)} fusion(bf16[2,196,3072]{2,0,1:T(2,128)(2,1)} %param.7, f32[3072]{0:T(1024)} %param.10, f32[2,3072]{1,0:T(2,128)S(1)} %sqrt_divide_fusion, f32[3072]{0:T(1024)} %param.9), kind=kLoop, calls=%fused_computation.7 | loop fusion | flops 7225344 | bytes 4866048 | tf_op jit(solution)/shard_map/convert_element_type | solution.py:23
  10.6 0.0 copy-done
  10.6 3.0 %bitcast_convert_fusion = bf16[3072,768]{1,0:T(8,128)(2,1)S(1)} fusion(bf16[2,196,3072]{2,0,1:T(2,128)(2,1)S(1)} %fusion.3, bf16[2,196,768]{2,0,1:T(2,128)(2,1)S(1)} %copy-done), kind=kOutput, calls=%fused_computation | convolution fusion | flops 1852047360 | bytes 7729152 | tf_op jit(solution)/shard_map/dot_general | solution.py:35
  13.6 0.0 copy-start.1
  13.6 2.1 %copy-done.1 = bf16[3072,768]{1,0:T(8,128)(2,1)} copy-done((bf16[3072,768]{1,0:T(8,128)(2,1)}, bf16[3072,768]{1,0:T(8,128)(2,1)S(1)}, u32[]{:S(2)}) %copy-start.1) | copy-done | bytes 4718616
  15.7 1.7 constant_dynamic-slice_fusion.1
  17.4 1.9 %collective-permute-start = (bf16[3072,384]{1,0:T(8,128)(2,1)}, bf16[3072,384]{1,0:T(8,128)(2,1)S(1)}, u32[]{:S(2)}, u32[]{:S(2)}) collective-permute-start(bf16[3072,384]{1,0:T(8,128)(2,1)} %constant_dynamic-slice_fusion.1), channel_id=1, source_target_pairs={{0,1},{1,0},{2,3},{3,2},{4,5},{5,4},{6,7},{7,6},{8,9},{9,8},{10,11... | collective-permute-start | bytes 7077896 | tf_op jit(solution)/shard_map/ppermute | solution.py:42
  19.3 4.7 %collective-permute-done = bf16[3072,384]{1,0:T(8,128)(2,1)S(1)} collective-permute-done((bf16[3072,384]{1,0:T(8,128)(2,1)}, bf16[3072,384]{1,0:T(8,128)(2,1)S(1)}, u32[]{:S(2)}, u32[]{:S(2)}) %collective-permute-start) | collective-permute-done | bytes 2359328 | tf_op jit(solution)/shard_map/ppermute | solution.py:42
  24.1 3.8 %add_convert_fusion = bf16[3072,384]{1,0:T(8,128)(2,1)} fusion(bf16[3072,384]{1,0:T(8,128)(2,1)S(1)} %collective-permute-done, bf16[3072,768]{1,0:T(8,128)(2,1)} %copy-done.1, s32[]{:T(128)S(6)} %select_n.37), kind=kLoop, calls=%fused_computation.9 | loop fusion | flops 4718592 | bytes 7077892 | tf_op jit(solution)/shard_map/convert_element_type | solution.py:46
  27.8 10.1 %all-to-all-start = ((bf16[16,192,384]{2,1,0:T(8,128)(2,1)}), bf16[16,192,384]{2,1,0:T(8,128)(2,1)S(1)}, u32[]{:S(2)}, u32[]{:S(2)}) async-start(bf16[16,192,384]{2,1,0:T(8,128)(2,1)} %bitcast.1), calls=%async_computation | async-start | bytes 4718592 | tf_op jit(solution)/shard_map/all_to_all | solution.py:45
  37.9 54.4 %all-to-all-done = bf16[16,192,384]{2,1,0:T(8,128)(2,1)S(1)} async-done(((bf16[16,192,384]{2,1,0:T(8,128)(2,1)}), bf16[16,192,384]{2,1,0:T(8,128)(2,1)S(1)}, u32[]{:S(2)}, u32[]{:S(2)}) %all-to-all-start) | async-done | bytes 2359328 | tf_op jit(solution)/shard_map/all_to_all | solution.py:45
  92.4 0.3 convert_reduce_fusion
  92.7 5.2 %collective-permute-start.1 = (f32[96,384]{1,0:T(8,128)S(1)}, f32[96,384]{1,0:T(8,128)S(1)}, u32[]{:S(2)}, u32[]{:S(2)}) collective-permute-start(f32[96,384]{1,0:T(8,128)S(1)} %constant_dynamic-slice_fusion), channel_id=1, source_target_pairs={{0,24},{24,0},{1,25},{25,1},{2,26},{26,2},{3,27},{27,3},{4,28},{28... | collective-permute-start | bytes 442376 | tf_op jit(solution)/shard_map/ppermute | solution.py:53
  97.9 3.1 %collective-permute-done.1 = f32[96,384]{1,0:T(8,128)S(1)} collective-permute-done((f32[96,384]{1,0:T(8,128)S(1)}, f32[96,384]{1,0:T(8,128)S(1)}, u32[]{:S(2)}, u32[]{:S(2)}) %collective-permute-start.1) | collective-permute-done | bytes 147488 | tf_op jit(solution)/shard_map/ppermute | solution.py:53
  101.0 25.3 %all_to_all.20 = f32[12,8,384]{2,1,0:T(8,128)S(1)} all-to-all(f32[12,8,384]{2,1,0:T(8,128)S(1)} %add_bitcast_fusion), channel_id=1, replica_groups=mesh['shard'=16,'xl'=2,'z'=12,'c'=2] {'z'}, dimensions={0} | all-to-all | bytes 294912 | tf_op jit(solution)/shard_map/all_to_all | solution.py:56
  126.4 14.8 %all_to_all.21 = f32[12,8,384]{2,1,0:T(8,128)S(1)} all-to-all(f32[12,8,384]{2,1,0:T(8,128)S(1)} %broadcast_in_dim.4), channel_id=1, replica_groups=mesh['shard'=16,'xl'=2,'z'=12,'c'=2] {'z'}, dimensions={0} | all-to-all | bytes 294912 | tf_op jit(solution)/shard_map/all_to_all | solution.py:59
  141.1 1.9 %collective-permute-start.2 = (f32[96,384]{1,0:T(8,128)S(1)}, f32[96,384]{1,0:T(8,128)S(1)}, u32[]{:S(2)}, u32[]{:S(2)}) collective-permute-start(f32[96,384]{1,0:T(8,128)S(1)} %bitcast.8), channel_id=1, source_target_pairs={{0,1},{1,0},{2,3},{3,2},{4,5},{5,4},{6,7},{7,6},{8,9},{9,8},{10,11... | collective-permute-start | bytes 442376 | tf_op jit(solution)/shard_map/ppermute | solution.py:61
  143.1 2.7 %collective-permute-start.3 = (f32[96,384]{1,0:T(8,128)S(1)}, f32[96,384]{1,0:T(8,128)S(1)}, u32[]{:S(2)}, u32[]{:S(2)}) collective-permute-start(f32[96,384]{1,0:T(8,128)S(1)} %bitcast.9), channel_id=1, source_target_pairs={{0,24},{24,0},{1,25},{25,1},{2,26},{26,2},{3,27},{27,3},{4,28},{28... | collective-permute-start | bytes 442376 | tf_op jit(solution)/shard_map/ppermute | solution.py:60
  145.8 2.9 %collective-permute-start.4 = (f32[96,384]{1,0:T(8,128)S(1)}, f32[96,384]{1,0:T(8,128)S(1)}, u32[]{:S(2)}, u32[]{:S(2)}) collective-permute-start(f32[96,384]{1,0:T(8,128)S(1)} %bitcast.10), channel_id=1, source_target_pairs={{0,25},{25,0},{1,24},{24,1},{2,27},{27,2},{3,26},{26,3},{4,29},{29... | collective-permute-start | bytes 442376 | tf_op jit(solution)/shard_map/ppermute | solution.py:62
  148.8 0.0 collective-permute-done.2
  148.8 2.9 %collective-permute-done.3 = f32[96,384]{1,0:T(8,128)S(1)} collective-permute-done((f32[96,384]{1,0:T(8,128)S(1)}, f32[96,384]{1,0:T(8,128)S(1)}, u32[]{:S(2)}, u32[]{:S(2)}) %collective-permute-start.3) | collective-permute-done | bytes 147488 | tf_op jit(solution)/shard_map/ppermute | solution.py:60
  151.7 2.2 %collective-permute-done.4 = f32[96,384]{1,0:T(8,128)S(1)} collective-permute-done((f32[96,384]{1,0:T(8,128)S(1)}, f32[96,384]{1,0:T(8,128)S(1)}, u32[]{:S(2)}, u32[]{:S(2)}) %collective-permute-start.4) | collective-permute-done | bytes 147488 | tf_op jit(solution)/shard_map/ppermute | solution.py:62
  153.9 2.9 %multiply_subtract_fusion = (f32[192,768]{1,0:T(8,128)S(1)}, f32[192,768]{1,0:T(8,128)}, f32[192,768]{1,0:T(8,128)}) fusion(f32[192,768]{1,0:T(8,128)} %param.11, f32[96,768]{1,0:T(8,128)S(1)} %maximum_select_fusion.1, f32[96,768]{1,0:T(8,128)S(1)} %maximum_select_fusion.2, pred[]{:T(512)S(6)} %eq.7, f32[192,768]{1,0:T(8,128)} %param.12, f32[192,768]{1,0:T(8,128)} %param.13), kind=kLoop, calls=%fused_computation.15 | loop fusion | flops 2654208 | bytes 4128769 | tf_op jit(solution)/shard_map/sub | solution.py:71
  156.8 0.0 copy-start.2
  156.8 0.1 dynamic-slice_convert_fusion
  156.9 0.1 copy.23
  157.0 17.7 %all_to_all.22 = bf16[16,192,16]{1,2,0:T(8,128)(2,1)S(1)} all-to-all(bf16[16,192,16]{1,2,0:T(8,128)(2,1)S(1)} %broadcast_in_dim.5), channel_id=1, replica_groups=mesh['shard'=16,'xl'=2,'z'=12,'c'=2] {'shard'}, dimensions={0} | all-to-all | bytes 196608 | tf_op jit(solution)/shard_map/all_to_all | solution.py:77
  174.7 0.8 reshape.50
  175.5 0.0 copy-done.2
  (9 shorter events, 0.2 us)
Async XLA Ops:
  0.6 10.0 %copy-start = (bf16[2,196,768]{2,0,1:T(2,128)(2,1)S(1)}, bf16[2,196,768]{2,0,1:T(2,128)(2,1)}, u32[]{:S(2)}) copy-start(bf16[2,196,768]{2,0,1:T(2,128)(2,1)} %param.8) | copy-start | bytes 1806340
  13.6 2.1 %copy-start.1 = (bf16[3072,768]{1,0:T(8,128)(2,1)}, bf16[3072,768]{1,0:T(8,128)(2,1)S(1)}, u32[]{:S(2)}) copy-start(bf16[3072,768]{1,0:T(8,128)(2,1)S(1)} %bitcast_convert_fusion) | copy-start | bytes 14155780
  17.4 6.6 %collective-permute-start = (bf16[3072,384]{1,0:T(8,128)(2,1)}, bf16[3072,384]{1,0:T(8,128)(2,1)S(1)}, u32[]{:S(2)}, u32[]{:S(2)}) collective-permute-start(bf16[3072,384]{1,0:T(8,128)(2,1)} %constant_dynamic-slice_fusion.1), channel_id=1, source_target_pairs={{0,1},{1,0},{2,3},{3,2},{4,5},{5,4},{6,7},{7,6},{8,9},{9,8},{10,11... | collective-permute-start | bytes 7077896 | tf_op jit(solution)/shard_map/ppermute | solution.py:42
  27.8 64.5 %all-to-all-start = ((bf16[16,192,384]{2,1,0:T(8,128)(2,1)}), bf16[16,192,384]{2,1,0:T(8,128)(2,1)S(1)}, u32[]{:S(2)}, u32[]{:S(2)}) async-start(bf16[16,192,384]{2,1,0:T(8,128)(2,1)} %bitcast.1), calls=%async_computation | async-start | bytes 4718592 | tf_op jit(solution)/shard_map/all_to_all | solution.py:45
  92.7 8.3 %collective-permute-start.1 = (f32[96,384]{1,0:T(8,128)S(1)}, f32[96,384]{1,0:T(8,128)S(1)}, u32[]{:S(2)}, u32[]{:S(2)}) collective-permute-start(f32[96,384]{1,0:T(8,128)S(1)} %constant_dynamic-slice_fusion), channel_id=1, source_target_pairs={{0,24},{24,0},{1,25},{25,1},{2,26},{26,2},{3,27},{27,3},{4,28},{28... | collective-permute-start | bytes 442376 | tf_op jit(solution)/shard_map/ppermute | solution.py:53
  141.1 7.6 %collective-permute-start.2 = (f32[96,384]{1,0:T(8,128)S(1)}, f32[96,384]{1,0:T(8,128)S(1)}, u32[]{:S(2)}, u32[]{:S(2)}) collective-permute-start(f32[96,384]{1,0:T(8,128)S(1)} %bitcast.8), channel_id=1, source_target_pairs={{0,1},{1,0},{2,3},{3,2},{4,5},{5,4},{6,7},{7,6},{8,9},{9,8},{10,11... | collective-permute-start | bytes 442376 | tf_op jit(solution)/shard_map/ppermute | solution.py:61
  143.1 8.6 %collective-permute-start.3 = (f32[96,384]{1,0:T(8,128)S(1)}, f32[96,384]{1,0:T(8,128)S(1)}, u32[]{:S(2)}, u32[]{:S(2)}) collective-permute-start(f32[96,384]{1,0:T(8,128)S(1)} %bitcast.9), channel_id=1, source_target_pairs={{0,24},{24,0},{1,25},{25,1},{2,26},{26,2},{3,27},{27,3},{4,28},{28... | collective-permute-start | bytes 442376 | tf_op jit(solution)/shard_map/ppermute | solution.py:60
  145.8 8.1 %collective-permute-start.4 = (f32[96,384]{1,0:T(8,128)S(1)}, f32[96,384]{1,0:T(8,128)S(1)}, u32[]{:S(2)}, u32[]{:S(2)}) collective-permute-start(f32[96,384]{1,0:T(8,128)S(1)} %bitcast.10), channel_id=1, source_target_pairs={{0,25},{25,0},{1,24},{24,1},{2,27},{27,2},{3,26},{26,3},{4,29},{29... | collective-permute-start | bytes 442376 | tf_op jit(solution)/shard_map/ppermute | solution.py:62
  156.8 18.7 %copy-start.2 = (f32[192,768]{1,0:T(8,128)}, f32[192,768]{1,0:T(8,128)S(1)}, u32[]{:S(2)}) copy-start(f32[192,768]{1,0:T(8,128)S(1)} %get-tuple-element.4) | copy-start | bytes 1769476

commit v3 on v2

--- a/solution.py
+++ b/solution.py
@@ -32,18 +32,28 @@
     channels = out_grad.shape[2]
     flat_rows = grn_forward(hidden_act, grn_gamma, grn_beta).reshape(images * positions, hidden)
     flat_grads = out_grad.reshape(images * positions, channels)
-    term = lax.dot_general(
-        flat_rows, flat_grads, (((0,), (0,)), ((), ())), preferred_element_type=jnp.float32
-    ).astype(jnp.bfloat16)
     core = lax.axis_index("c")
     half = channels // CORES
-    mine = lax.dynamic_slice_in_dim(term, core * half, half, 1)
-    other = lax.dynamic_slice_in_dim(term, (1 - core) * half, half, 1)
-    chip = mine.astype(jnp.float32) + lax.ppermute(other, "c", SWAP).astype(jnp.float32)
-    n_shard = lax.axis_size("shard")
+
+    def term_of(start):
+        cols = lax.dynamic_slice_in_dim(flat_grads, start, half, 1)
+        return lax.dot_general(
+            flat_rows, cols, (((0,), (0,)), ((), ())), preferred_element_type=jnp.float32
+        ).astype(jnp.bfloat16)
+
+    sent = lax.ppermute(term_of((1 - core) * half), "c", SWAP)
+    chip = term_of(core * half).astype(jnp.float32) + sent.astype(jnp.float32)
+    n_shard = lax.axis_size(("xh", "y"))
+    n_xh = lax.axis_size("xh")
+    n_y = lax.axis_size("y")
     block = hidden // n_shard
+    x_hi = lax.axis_index("xh")
+    wide = hidden // n_xh
+    keep = lax.dynamic_slice_in_dim(chip, x_hi * wide, wide, 0)
+    give = lax.dynamic_slice_in_dim(chip.astype(jnp.bfloat16), (1 - x_hi) * wide, wide, 0)
+    pair = keep + lax.ppermute(give, "xh", SWAP).astype(jnp.float32)
     pieces = lax.all_to_all(
-        chip.astype(jnp.bfloat16).reshape(n_shard, block, half), "shard", 0, 0, tiled=True
+        pair.astype(jnp.bfloat16).reshape(n_y, block, half), "y", 0, 0, tiled=True
     )
     part = jnp.sum(pieces.astype(jnp.float32), axis=0)
     x_lo = lax.axis_index("xl")
@@ -74,24 +84,24 @@
     own_start = lax.axis_index(("xl", "z", "c")) * own_width
     own_columns = lax.dynamic_slice_in_dim(new_master.astype(jnp.bfloat16), own_start, own_width, 1)
     spread_cols = jnp.broadcast_to(own_columns[None], (n_shard, block, own_width))
-    weights = lax.all_to_all(spread_cols, "shard", 0, 0, tiled=True).reshape(hidden, own_width)
+    weights = lax.all_to_all(spread_cols, ("xh", "y"), 0, 0, tiled=True).reshape(hidden, own_width)
     return (new_master, new_moment_one, new_moment_two, weights)
 
 
 def solution(mesh):
     n_shard, n_rep = mesh.shape["shard"], mesh.shape["rep"]
-    x_lo = 2
-    devices = np.asarray(mesh.devices).reshape(n_shard, x_lo, n_rep // (x_lo * CORES), CORES)
-    fine = Mesh(devices, ("shard", "xl", "z", "c"))
-    rows = ("shard", "xl", "z", "c")
+    x_hi = x_lo = 2
+    devices = np.asarray(mesh.devices).reshape(x_hi, n_shard // x_hi, x_lo, n_rep // (x_lo * CORES), CORES)
+    fine = Mesh(devices, ("xh", "y", "xl", "z", "c"))
+    rows = ("xh", "y", "xl", "z", "c")
     in_specs = (
         P(rows, None, None),
         P(rows, None, None),
         P(),
         P(),
-        P("shard", None),
-        P("shard", None),
-        P("shard", None),
+        P(("xh", "y"), None),
+        P(("xh", "y"), None),
+        P(("xh", "y"), None),
     )
-    out_specs = (P("shard", None), P("shard", None), P("shard", None), P(None, ("xl", "z", "c")))
+    out_specs = (P(("xh", "y"), None), P(("xh", "y"), None), P(("xh", "y"), None), P(None, ("xl", "z", "c")))
     return jax.shard_map(body, mesh=fine, in_specs=in_specs, out_specs=out_specs, check_vma=False)

time: 178 us -> 185 us (1.039)
  blocking collectives: 57.8 us -> 51.7 us
  waiting for transfers between devices: 67.3 us -> 72.8 us
  matrix products: 3 us -> 7.96 us
  local copies, waits for them, and re-layouts: 4.86 us -> 9.63 us
  other arithmetic: 17 us -> 13 us
    ppermute x1 -> x2, waiting for transfers between devices: 4.71 us -> 32.7 us  [the longest x1 27.9 us: body(): pair = keep + lax.ppermute(give, 'xh', SWAP).astype(jnp.float32)]
    all_to_all x1, waiting for transfers between devices: 54.4 us -> 31 us  [body(): lax.all_to_all(pair.astype(jnp.bfloat16).reshape(n_y, block, half), 'y',...]
    all_to_all x1, blocking collectives: 17.7 us -> 12.6 us  [body(): lax.all_to_all(spread_cols, ('xh', 'y'), 0, 0, tiled=True)]
    dot_general x1 -> x2, matrix products: 3 us -> 7.96 us  [term_of(): lax.dot_general(flat_rows, cols, (((0,), (0,)), ((), ())), preferred_elem...]
    ppermute x1 -> x2, starting transfers between devices: 1.91 us -> 5.41 us  [the longest x1 3.5 us: body(): pair = keep + lax.ppermute(give, 'xh', SWAP).astype(jnp.float32)]
    reshape x1 -> x3, local copies, waits for them, and re-layouts: 0.81 us -> 3.91 us  [the longest x1 2.17 us: body(): grn_forward(hidden_act, grn_gamma, grn_beta)]
    all_to_all x1, starting transfers between devices: 10.1 us -> 7.1 us  [body(): lax.all_to_all(pair.astype(jnp.bfloat16).reshape(n_y, block, half), 'y',...]
    convert_element_type x0 -> x2, local copies, waits for them, and re-layouts: none -> 2.18 us  [the longest x1 2.05 us: grn_forward(): return grn_out.astype(jnp.bfloat16)]
  transfers between devices with their start and end apart: 6 -> 7, of which waited for: 5 -> 6; matrix products, arithmetic and copies ran while one was open for 0% -> 0% of each run, Pallas kernels for 0% -> 0%
where the time goes in v3:
time: 185 us; the launch traced here: 182 us
  waiting for transfers between devices  72.8 us (39%)
  blocking collectives  51.7 us (28%)
  starting transfers between devices  26.1 us (14%)
  other arithmetic  13 us (7%)
  local copies, waits for them, and re-layouts  9.63 us (5%)
  matrix products  7.96 us (4%)
    all_to_all x1, waiting for transfers between devices, body(): lax.all_to_all(pair.astype(jnp.bfloat16).reshape(n_y, block, half), 'y',...  31 us
    ppermute x1, waiting for transfers between devices, body(): pair = keep + lax.ppermute(give, 'xh', SWAP).astype(jnp.float32)  27.9 us
    all_to_all x1, blocking collectives, body(): lax.all_to_all(part_half.reshape(n_z, sub, half), 'z', 0, 0, tiled=True)  24.8 us
    all_to_all x1, blocking collectives, body(): lax.all_to_all(spread, 'z', 0, 0, tiled=True).reshape(rows_half, half)  14.3 us
    all_to_all x1, blocking collectives, body(): lax.all_to_all(spread_cols, ('xh', 'y'), 0, 0, tiled=True)  12.6 us
    dot_general x2, matrix products, term_of(): lax.dot_general(flat_rows, cols, (((0,), (0,)), ((), ())), preferred_elem...  7.96 us
    all_to_all x1, starting transfers between devices, body(): lax.all_to_all(pair.astype(jnp.bfloat16).reshape(n_y, block, half), 'y',...  7.1 us
    ppermute x1, starting transfers between devices, body(): part_half = mine_rows + lax.ppermute(other_rows, 'xl', SWAP)  5.98 us
  transfers between devices with their start and end apart: 7, of which 6 were waited for; matrix products, arithmetic and copies ran while one was open for 0% of the time, Pallas kernels for 0%

profile of v3, /device:TPU:6, one launch (start us, length us, event | category | flops | bytes accessed | tf_op | source)
XLA Modules:
  0.0 182.1 jit_solution(11714481155571028581)
XLA Ops:
  0.6 0.0 copy-start.1
  0.6 0.0 copy-start.7
  0.7 0.0 copy-start.8
  0.7 4.4 %fusion = f32[2,3072]{1,0:T(2,128)S(1)} fusion(bf16[2,196,3072]{2,0,1:T(2,128)(2,1)} %param.7), kind=kLoop, calls=%fused_computation.3 | loop fusion | flops 3606528 | bytes 2433024 | tf_op jit(solution)/shard_map/reduce_sum | solution.py:20
  5.1 0.1 sqrt_reduce_fusion
  5.2 0.1 sqrt_divide_fusion
  5.3 0.0 copy-done.1
  5.3 0.0 copy-done.7
  5.3 0.0 copy-done.8
  5.3 3.7 %fusion.3 = bf16[2,196,3072]{2,0,1:T(2,128)(2,1)S(1)} fusion(bf16[2,196,3072]{2,0,1:T(2,128)(2,1)S(1)} %copy-done.1, f32[3072]{0:T(1024)S(1)} %copy-done.7, f32[2,3072]{1,0:T(2,128)S(1)} %sqrt_divide_fusion, f32[3072]{0:T(1024)S(1)} %copy-done.8), kind=kLoop, calls=%fused_computation.6 | loop fusion | flops 7225344 | bytes 4866048 | tf_op jit(solution)/shard_map/convert_element_type | solution.py:23
  9.0 2.1 %copy.22 = bf16[2,196,3072]{2,1,0:T(8,128)(2,1)} copy(bf16[2,196,3072]{2,0,1:T(2,128)(2,1)S(1)} %fusion.3) | data formatting | bytes 4816896 | tf_op jit(solution)/shard_map/convert_element_type | solution.py:23
  11.1 2.2 %reshape.51 = bf16[392,3072]{1,0:T(8,128)(2,1)S(1)} reshape(bf16[2,196,3072]{2,1,0:T(8,128)(2,1)} %copy.22) | data formatting | bytes 4816896 | tf_op jit(solution)/shard_map/reshape | solution.py:33
  13.3 1.1 copy.23
  14.4 0.9 reshape.52
  15.3 0.0 copy-start.2
  15.3 4.3 %convolution_convert_fusion = bf16[3072,384]{1,0:T(8,128)(2,1)} fusion(bf16[392,3072]{1,0:T(8,128)(2,1)S(1)} %reshape.51, bf16[392,768]{1,0:T(8,128)(2,1)} %reshape.52, s32[]{:T(128)S(6)} %select_n.44), kind=kOutput, calls=%fused_computation.8 | convolution fusion | flops 926023680 | bytes 5068804 | tf_op jit(solution)/shard_map/dot_general | solution.py:40
  19.7 1.9 %collective-permute-start = (bf16[3072,384]{1,0:T(8,128)(2,1)}, bf16[3072,384]{1,0:T(8,128)(2,1)}, u32[]{:S(2)}, u32[]{:S(2)}) collective-permute-start(bf16[3072,384]{1,0:T(8,128)(2,1)} %convolution_convert_fusion), channel_id=1, source_target_pairs={{0,1},{1,0},{2,3},{3,2},{4,5},{5,4},{6,7},{7,6},{8,9},{9,8},{10,11... | collective-permute-start | bytes 7077896 | tf_op jit(solution)/shard_map/ppermute | solution.py:44
  21.6 4.8 %collective-permute-done = bf16[3072,384]{1,0:T(8,128)(2,1)} collective-permute-done((bf16[3072,384]{1,0:T(8,128)(2,1)}, bf16[3072,384]{1,0:T(8,128)(2,1)}, u32[]{:S(2)}, u32[]{:S(2)}) %collective-permute-start) | collective-permute-done | bytes 2359328 | tf_op jit(solution)/shard_map/ppermute | solution.py:44
  26.4 0.0 copy-done.2
  26.4 3.6 %convert_add_fusion.1 = f32[3072,384]{1,0:T(8,128)S(1)} fusion(bf16[3072,384]{1,0:T(8,128)(2,1)} %collective-permute-done, bf16[392,3072]{1,0:T(8,128)(2,1)S(1)} %reshape.51, bf16[392,768]{1,0:T(8,128)(2,1)S(1)} %copy-done.2, s32[]{:T(128)S(6)} %select_n.43), kind=kOutput, calls=%fused_computation.7 | convolution fusion | flops 929562624 | bytes 9787396 | tf_op jit(solution)/shard_map/dot_general | solution.py:40
  30.1 0.0 copy-start
  30.1 2.1 %copy-done = f32[3072,384]{1,0:T(8,128)} copy-done((f32[3072,384]{1,0:T(8,128)}, f32[3072,384]{1,0:T(8,128)S(1)}, u32[]{:S(2)}) %copy-start) | copy-done | bytes 4718616
  32.2 0.1 dynamic-slice_convert_fusion
  32.3 3.5 %collective-permute-start.1 = (bf16[1536,384]{1,0:T(8,128)(2,1)S(1)}, bf16[1536,384]{1,0:T(8,128)(2,1)S(1)}, u32[]{:S(2)}, u32[]{:S(2)}) collective-permute-start(bf16[1536,384]{1,0:T(8,128)(2,1)S(1)} %dynamic-slice_convert_fusion), channel_id=1, source_target_pairs={{0,384},{384,0},{1,385},{385,1},{2,386},{386,2},{3,387},{387,3},{4... | collective-permute-start | bytes 3538952 | tf_op jit(solution)/shard_map/ppermute | solution.py:54
  35.8 27.9 %collective-permute-done.1 = bf16[1536,384]{1,0:T(8,128)(2,1)S(1)} collective-permute-done((bf16[1536,384]{1,0:T(8,128)(2,1)S(1)}, bf16[1536,384]{1,0:T(8,128)(2,1)S(1)}, u32[]{:S(2)}, u32[]{:S(2)}) %collective-permute-start.1) | collective-permute-done | bytes 1179680 | tf_op jit(solution)/shard_map/ppermute | solution.py:54
  63.8 3.0 %add_convert_fusion = bf16[1536,384]{1,0:T(8,128)(2,1)} fusion(bf16[1536,384]{1,0:T(8,128)(2,1)S(1)} %collective-permute-done.1, f32[3072,384]{1,0:T(8,128)} %copy-done, s32[]{:T(128)S(6)} %select_n.45), kind=kLoop, calls=%fused_computation.12 | loop fusion | flops 1769472 | bytes 4718596 | tf_op jit(solution)/shard_map/convert_element_type | solution.py:56
  66.7 7.1 %all-to-all-start = ((bf16[8,192,384]{2,1,0:T(8,128)(2,1)}), bf16[8,192,384]{2,1,0:T(8,128)(2,1)S(1)}, u32[]{:S(2)}, u32[]{:S(2)}) async-start(bf16[8,192,384]{2,1,0:T(8,128)(2,1)} %bitcast), calls=%async_computation | async-start | bytes 2359296 | tf_op jit(solution)/shard_map/all_to_all | solution.py:55
  73.8 0.0 copy-start.4
  73.8 0.0 copy-start.5
  73.9 0.0 copy-start.6
  73.9 31.0 %all-to-all-done = bf16[8,192,384]{2,1,0:T(8,128)(2,1)S(1)} async-done(((bf16[8,192,384]{2,1,0:T(8,128)(2,1)}), bf16[8,192,384]{2,1,0:T(8,128)(2,1)S(1)}, u32[]{:S(2)}, u32[]{:S(2)}) %all-to-all-start) | async-done | bytes 1179680 | tf_op jit(solution)/shard_map/all_to_all | solution.py:55
  104.8 0.2 convert_reduce_fusion
  105.0 6.0 %collective-permute-start.2 = (f32[96,384]{1,0:T(8,128)S(1)}, f32[96,384]{1,0:T(8,128)S(1)}, u32[]{:S(2)}, u32[]{:S(2)}) collective-permute-start(f32[96,384]{1,0:T(8,128)S(1)} %constant_dynamic-slice_fusion), channel_id=1, source_target_pairs={{0,24},{24,0},{1,25},{25,1},{2,26},{26,2},{3,27},{27,3},{4,28},{28... | collective-permute-start | bytes 442376 | tf_op jit(solution)/shard_map/ppermute | solution.py:63
  111.0 4.0 %collective-permute-done.2 = f32[96,384]{1,0:T(8,128)S(1)} collective-permute-done((f32[96,384]{1,0:T(8,128)S(1)}, f32[96,384]{1,0:T(8,128)S(1)}, u32[]{:S(2)}, u32[]{:S(2)}) %collective-permute-start.2) | collective-permute-done | bytes 147488 | tf_op jit(solution)/shard_map/ppermute | solution.py:63
  115.0 24.8 %all_to_all.20 = f32[12,8,384]{2,1,0:T(8,128)S(1)} all-to-all(f32[12,8,384]{2,1,0:T(8,128)S(1)} %add_bitcast_fusion), channel_id=1, replica_groups=mesh['xh'=2,'y'=8,'xl'=2,'z'=12,'c'=2] {'z'}, dimensions={0} | all-to-all | bytes 294912 | tf_op jit(solution)/shard_map/all_to_all | solution.py:66
  139.9 14.3 %all_to_all.21 = f32[12,8,384]{2,1,0:T(8,128)S(1)} all-to-all(f32[12,8,384]{2,1,0:T(8,128)S(1)} %broadcast_in_dim.4), channel_id=1, replica_groups=mesh['xh'=2,'y'=8,'xl'=2,'z'=12,'c'=2] {'z'}, dimensions={0} | all-to-all | bytes 294912 | tf_op jit(solution)/shard_map/all_to_all | solution.py:69
  154.2 1.9 %collective-permute-start.3 = (f32[96,384]{1,0:T(8,128)S(1)}, f32[96,384]{1,0:T(8,128)S(1)}, u32[]{:S(2)}, u32[]{:S(2)}) collective-permute-start(f32[96,384]{1,0:T(8,128)S(1)} %bitcast.8), channel_id=1, source_target_pairs={{0,1},{1,0},{2,3},{3,2},{4,5},{5,4},{6,7},{7,6},{8,9},{9,8},{10,11... | collective-permute-start | bytes 442376 | tf_op jit(solution)/shard_map/ppermute | solution.py:71
  156.1 2.7 %collective-permute-start.4 = (f32[96,384]{1,0:T(8,128)S(1)}, f32[96,384]{1,0:T(8,128)S(1)}, u32[]{:S(2)}, u32[]{:S(2)}) collective-permute-start(f32[96,384]{1,0:T(8,128)S(1)} %bitcast.9), channel_id=1, source_target_pairs={{0,24},{24,0},{1,25},{25,1},{2,26},{26,2},{3,27},{27,3},{4,28},{28... | collective-permute-start | bytes 442376 | tf_op jit(solution)/shard_map/ppermute | solution.py:70
  158.8 2.9 %collective-permute-start.5 = (f32[96,384]{1,0:T(8,128)S(1)}, f32[96,384]{1,0:T(8,128)S(1)}, u32[]{:S(2)}, u32[]{:S(2)}) collective-permute-start(f32[96,384]{1,0:T(8,128)S(1)} %bitcast.10), channel_id=1, source_target_pairs={{0,25},{25,0},{1,24},{24,1},{2,27},{27,2},{3,26},{26,3},{4,29},{29... | collective-permute-start | bytes 442376 | tf_op jit(solution)/shard_map/ppermute | solution.py:72
  161.8 0.0 collective-permute-done.3
  161.8 2.9 %collective-permute-done.4 = f32[96,384]{1,0:T(8,128)S(1)} collective-permute-done((f32[96,384]{1,0:T(8,128)S(1)}, f32[96,384]{1,0:T(8,128)S(1)}, u32[]{:S(2)}, u32[]{:S(2)}) %collective-permute-start.4) | collective-permute-done | bytes 147488 | tf_op jit(solution)/shard_map/ppermute | solution.py:70
  164.7 2.2 %collective-permute-done.5 = f32[96,384]{1,0:T(8,128)S(1)} collective-permute-done((f32[96,384]{1,0:T(8,128)S(1)}, f32[96,384]{1,0:T(8,128)S(1)}, u32[]{:S(2)}, u32[]{:S(2)}) %collective-permute-start.5) | collective-permute-done | bytes 147488 | tf_op jit(solution)/shard_map/ppermute | solution.py:72
  166.9 0.0 copy-done.4
  167.0 0.0 copy-done.5
  167.0 0.0 copy-done.6
  167.0 1.5 multiply_subtract_fusion
  168.4 0.0 copy-start.3
  168.5 0.1 dynamic-slice_convert_fusion.1
  168.5 0.1 copy.24
  168.6 12.6 %all_to_all.22 = bf16[16,192,16]{1,2,0:T(8,128)(2,1)S(1)} all-to-all(bf16[16,192,16]{1,2,0:T(8,128)(2,1)S(1)} %broadcast_in_dim.5), channel_id=1, replica_groups=mesh['xh'=2,'y'=8,'xl'=2,'z'=12,'c'=2] {'xh','y'}, dimensions={0} | all-to-all | bytes 196608 | tf_op jit(solution)/shard_map/all_to_all | solution.py:87
  181.3 0.8 reshape.56
  182.1 0.0 copy-done.3
  (9 shorter events, 0.2 us)
Async XLA Ops:
  0.6 4.7 %copy-start.1 = (bf16[2,196,3072]{2,0,1:T(2,128)(2,1)S(1)}, bf16[2,196,3072]{2,0,1:T(2,128)(2,1)}, u32[]{:S(2)}) copy-start(bf16[2,196,3072]{2,0,1:T(2,128)(2,1)} %param.7) | copy-start | bytes 7225348
  0.6 4.7 %copy-start.7 = (f32[3072]{0:T(1024)S(1)}, f32[3072]{0:T(1024)}, u32[]{:S(2)}) copy-start(f32[3072]{0:T(1024)} %param.10) | copy-start | bytes 36868
  0.7 4.7 %copy-start.8 = (f32[3072]{0:T(1024)S(1)}, f32[3072]{0:T(1024)}, u32[]{:S(2)}) copy-start(f32[3072]{0:T(1024)} %param.9) | copy-start | bytes 36868
  15.3 11.1 %copy-start.2 = (bf16[392,768]{1,0:T(8,128)(2,1)S(1)}, bf16[392,768]{1,0:T(8,128)(2,1)}, u32[]{:S(2)}) copy-start(bf16[392,768]{1,0:T(8,128)(2,1)} %reshape.52) | copy-start | bytes 1806340
  19.7 6.8 %collective-permute-start = (bf16[3072,384]{1,0:T(8,128)(2,1)}, bf16[3072,384]{1,0:T(8,128)(2,1)}, u32[]{:S(2)}, u32[]{:S(2)}) collective-permute-start(bf16[3072,384]{1,0:T(8,128)(2,1)} %convolution_convert_fusion), channel_id=1, source_target_pairs={{0,1},{1,0},{2,3},{3,2},{4,5},{5,4},{6,7},{7,6},{8,9},{9,8},{10,11... | collective-permute-start | bytes 7077896 | tf_op jit(solution)/shard_map/ppermute | solution.py:44
  30.1 2.1 %copy-start = (f32[3072,384]{1,0:T(8,128)}, f32[3072,384]{1,0:T(8,128)S(1)}, u32[]{:S(2)}) copy-start(f32[3072,384]{1,0:T(8,128)S(1)} %convert_add_fusion.1) | copy-start | bytes 14155780
  32.3 31.4 %collective-permute-start.1 = (bf16[1536,384]{1,0:T(8,128)(2,1)S(1)}, bf16[1536,384]{1,0:T(8,128)(2,1)S(1)}, u32[]{:S(2)}, u32[]{:S(2)}) collective-permute-start(bf16[1536,384]{1,0:T(8,128)(2,1)S(1)} %dynamic-slice_convert_fusion), channel_id=1, source_target_pairs={{0,384},{384,0},{1,385},{385,1},{2,386},{386,2},{3,387},{387,3},{4... | collective-permute-start | bytes 3538952 | tf_op jit(solution)/shard_map/ppermute | solution.py:54
  66.7 38.1 %all-to-all-start = ((bf16[8,192,384]{2,1,0:T(8,128)(2,1)}), bf16[8,192,384]{2,1,0:T(8,128)(2,1)S(1)}, u32[]{:S(2)}, u32[]{:S(2)}) async-start(bf16[8,192,384]{2,1,0:T(8,128)(2,1)} %bitcast), calls=%async_computation | async-start | bytes 2359296 | tf_op jit(solution)/shard_map/all_to_all | solution.py:55
  73.8 93.1 %copy-start.4 = (f32[192,768]{1,0:T(8,128)S(1)}, f32[192,768]{1,0:T(8,128)}, u32[]{:S(2)}) copy-start(f32[192,768]{1,0:T(8,128)} %param.11) | copy-start | bytes 1769476
  73.8 93.1 %copy-start.5 = (f32[192,768]{1,0:T(8,128)S(1)}, f32[192,768]{1,0:T(8,128)}, u32[]{:S(2)}) copy-start(f32[192,768]{1,0:T(8,128)} %param.12) | copy-start | bytes 1769476
  73.9 93.1 %copy-start.6 = (f32[192,768]{1,0:T(8,128)S(1)}, f32[192,768]{1,0:T(8,128)}, u32[]{:S(2)}) copy-start(f32[192,768]{1,0:T(8,128)} %param.13) | copy-start | bytes 1769476
  105.0 10.0 %collective-permute-start.2 = (f32[96,384]{1,0:T(8,128)S(1)}, f32[96,384]{1,0:T(8,128)S(1)}, u32[]{:S(2)}, u32[]{:S(2)}) collective-permute-start(f32[96,384]{1,0:T(8,128)S(1)} %constant_dynamic-slice_fusion), channel_id=1, source_target_pairs={{0,24},{24,0},{1,25},{25,1},{2,26},{26,2},{3,27},{27,3},{4,28},{28... | collective-permute-start | bytes 442376 | tf_op jit(solution)/shard_map/ppermute | solution.py:63
  154.2 7.6 %collective-permute-start.3 = (f32[96,384]{1,0:T(8,128)S(1)}, f32[96,384]{1,0:T(8,128)S(1)}, u32[]{:S(2)}, u32[]{:S(2)}) collective-permute-start(f32[96,384]{1,0:T(8,128)S(1)} %bitcast.8), channel_id=1, source_target_pairs={{0,1},{1,0},{2,3},{3,2},{4,5},{5,4},{6,7},{7,6},{8,9},{9,8},{10,11... | collective-permute-start | bytes 442376 | tf_op jit(solution)/shard_map/ppermute | solution.py:71
  156.1 8.6 %collective-permute-start.4 = (f32[96,384]{1,0:T(8,128)S(1)}, f32[96,384]{1,0:T(8,128)S(1)}, u32[]{:S(2)}, u32[]{:S(2)}) collective-permute-start(f32[96,384]{1,0:T(8,128)S(1)} %bitcast.9), channel_id=1, source_target_pairs={{0,24},{24,0},{1,25},{25,1},{2,26},{26,2},{3,27},{27,3},{4,28},{28... | collective-permute-start | bytes 442376 | tf_op jit(solution)/shard_map/ppermute | solution.py:70
  158.8 8.1 %collective-permute-start.5 = (f32[96,384]{1,0:T(8,128)S(1)}, f32[96,384]{1,0:T(8,128)S(1)}, u32[]{:S(2)}, u32[]{:S(2)}) collective-permute-start(f32[96,384]{1,0:T(8,128)S(1)} %bitcast.10), channel_id=1, source_target_pairs={{0,25},{25,0},{1,24},{24,1},{2,27},{27,2},{3,26},{26,3},{4,29},{29... | collective-permute-start | bytes 442376 | tf_op jit(solution)/shard_map/ppermute | solution.py:72
  168.4 13.6 %copy-start.3 = (f32[192,768]{1,0:T(8,128)}, f32[192,768]{1,0:T(8,128)S(1)}, u32[]{:S(2)}) copy-start(f32[192,768]{1,0:T(8,128)S(1)} %get-tuple-element.4) | copy-start | bytes 1769476

commit v4 on v2

--- a/solution.py
+++ b/solution.py
@@ -48,12 +48,10 @@
     part = jnp.sum(pieces.astype(jnp.float32), axis=0)
     x_lo = lax.axis_index("xl")
     rows_half = block // 2
-    mine_rows = lax.dynamic_slice_in_dim(part, x_lo * rows_half, rows_half, 0)
-    other_rows = lax.dynamic_slice_in_dim(part, (1 - x_lo) * rows_half, rows_half, 0)
-    part_half = mine_rows + lax.ppermute(other_rows, "xl", SWAP)
     n_z = lax.axis_size("z")
-    sub = rows_half // n_z
-    pieces2 = lax.all_to_all(part_half.reshape(n_z, sub, half), "z", 0, 0, tiled=True)
+    n_xz = lax.axis_size(("xl", "z"))
+    sub = block // n_xz
+    pieces2 = lax.all_to_all(part.reshape(n_xz, sub, half), ("xl", "z"), 0, 0, tiled=True)
     grad_sub = jnp.sum(pieces2, axis=0)
     spread = jnp.broadcast_to(grad_sub[None], (n_z, sub, half))
     grad_quarter = lax.all_to_all(spread, "z", 0, 0, tiled=True).reshape(rows_half, half)

time: 178 us -> 172 us (0.966)
  blocking collectives: 57.8 us -> 127 us
  waiting for transfers between devices: 67.3 us -> 10.2 us
  starting transfers between devices: 24.7 us -> 9.48 us
  other arithmetic: 17 us -> 14.2 us
    all_to_all x1 -> x2, blocking collectives: 25.3 us -> 94.4 us  [the longest x1 64.7 us: body(): lax.all_to_all(chip.astype(jnp.bfloat16).reshape(n_shard, block, half), '...]
    all_to_all x1 -> x0, waiting for transfers between devices: 54.4 us -> none  [body(): lax.all_to_all(chip.astype(jnp.bfloat16).reshape(n_shard, block, half), '...]
    all_to_all x1 -> x0, starting transfers between devices: 10.1 us -> none  [body(): lax.all_to_all(chip.astype(jnp.bfloat16).reshape(n_shard, block, half), '...]
    ppermute x1 -> x0, starting transfers between devices: 5.15 us -> none  [body(): part_half = mine_rows + lax.ppermute(other_rows, 'xl', SWAP)]
    ppermute x1 -> x0, waiting for transfers between devices: 3.1 us -> none  [body(): part_half = mine_rows + lax.ppermute(other_rows, 'xl', SWAP)]
  transfers between devices with their start and end apart: 6 -> 4, of which waited for: 5 -> 3; matrix products, arithmetic and copies ran while one was open for 0% -> 0% of each run, Pallas kernels for 0% -> 0%
where the time goes in v4:
time: 172 us; the launch traced here: 170 us
  blocking collectives  127 us (74%)
  other arithmetic  14.2 us (8%)
  waiting for transfers between devices  10.2 us (6%)
  starting transfers between devices  9.48 us (6%)
  local copies, waits for them, and re-layouts  4.87 us (3%)
  matrix products  3 us (2%)
    all_to_all x1, blocking collectives, body(): lax.all_to_all(chip.astype(jnp.bfloat16).reshape(n_shard, block, half), '...  64.7 us
    all_to_all x1, blocking collectives, body(): lax.all_to_all(part.reshape(n_xz, sub, half), ('xl', 'z'), 0, 0, tiled=True)  29.7 us
    all_to_all x1, blocking collectives, body(): lax.all_to_all(spread_cols, 'shard', 0, 0, tiled=True)  17.1 us
    all_to_all x1, blocking collectives, body(): lax.all_to_all(spread, 'z', 0, 0, tiled=True).reshape(rows_half, half)  15.8 us
    convert_element_type x1, other arithmetic, grn_forward(): return grn_out.astype(jnp.bfloat16)  5.42 us
    ppermute x1, waiting for transfers between devices, body(): lax.ppermute(other, 'c', SWAP).astype(jnp.float32)  4.71 us
    reduce_sum x1, other arithmetic, grn_forward(): spatial_norm = jnp.sqrt(jnp.sum(values * values, axis=1))  4.29 us
    ppermute x1, starting transfers between devices, body(): from_x = lax.ppermute(grad_quarter, 'xl', SWAP)  3.57 us
  transfers between devices with their start and end apart: 4, of which 3 were waited for; matrix products, arithmetic and copies ran while one was open for 0% of the time, Pallas kernels for 0%

profile of v4, /device:TPU:6, one launch (start us, length us, event | category | flops | bytes accessed | tf_op | source)
XLA Modules:
  0.0 169.9 jit_solution(2853881954342308832)
XLA Ops:
  0.6 0.0 copy-start
  0.7 4.3 %fusion = f32[2,3072]{1,0:T(2,128)S(1)} fusion(bf16[2,196,3072]{2,0,1:T(2,128)(2,1)} %param.7), kind=kLoop, calls=%fused_computation.4 | loop fusion | flops 3606528 | bytes 2433024 | tf_op jit(solution)/shard_map/reduce_sum | solution.py:20
  4.9 0.1 sqrt_reduce_fusion
  5.1 0.1 sqrt_divide_fusion
  5.2 5.4 %fusion.3 = bf16[2,196,3072]{2,0,1:T(2,128)(2,1)S(1)} fusion(bf16[2,196,3072]{2,0,1:T(2,128)(2,1)} %param.7, f32[3072]{0:T(1024)} %param.10, f32[2,3072]{1,0:T(2,128)S(1)} %sqrt_divide_fusion, f32[3072]{0:T(1024)} %param.9), kind=kLoop, calls=%fused_computation.7 | loop fusion | flops 7225344 | bytes 4866048 | tf_op jit(solution)/shard_map/convert_element_type | solution.py:23
  10.6 0.0 copy-done
  10.6 3.0 %bitcast_convert_fusion = bf16[3072,768]{1,0:T(8,128)(2,1)S(1)} fusion(bf16[2,196,3072]{2,0,1:T(2,128)(2,1)S(1)} %fusion.3, bf16[2,196,768]{2,0,1:T(2,128)(2,1)S(1)} %copy-done), kind=kOutput, calls=%fused_computation | convolution fusion | flops 1852047360 | bytes 7729152 | tf_op jit(solution)/shard_map/dot_general | solution.py:35
  13.6 0.0 copy-start.1
  13.6 2.1 %copy-done.1 = bf16[3072,768]{1,0:T(8,128)(2,1)} copy-done((bf16[3072,768]{1,0:T(8,128)(2,1)}, bf16[3072,768]{1,0:T(8,128)(2,1)S(1)}, u32[]{:S(2)}) %copy-start.1) | copy-done | bytes 4718616
  15.7 1.7 constant_dynamic-slice_fusion
  17.4 1.9 %collective-permute-start = (bf16[3072,384]{1,0:T(8,128)(2,1)}, bf16[3072,384]{1,0:T(8,128)(2,1)S(1)}, u32[]{:S(2)}, u32[]{:S(2)}) collective-permute-start(bf16[3072,384]{1,0:T(8,128)(2,1)} %constant_dynamic-slice_fusion), channel_id=1, source_target_pairs={{0,1},{1,0},{2,3},{3,2},{4,5},{5,4},{6,7},{7,6},{8,9},{9,8},{10,11... | collective-permute-start | bytes 7077896 | tf_op jit(solution)/shard_map/ppermute | solution.py:42
  19.3 4.7 %collective-permute-done = bf16[3072,384]{1,0:T(8,128)(2,1)S(1)} collective-permute-done((bf16[3072,384]{1,0:T(8,128)(2,1)}, bf16[3072,384]{1,0:T(8,128)(2,1)S(1)}, u32[]{:S(2)}, u32[]{:S(2)}) %collective-permute-start) | collective-permute-done | bytes 2359328 | tf_op jit(solution)/shard_map/ppermute | solution.py:42
  24.1 2.3 %add_convert_fusion = bf16[3072,384]{1,0:T(8,128)(2,1)S(1)} fusion(bf16[3072,384]{1,0:T(8,128)(2,1)S(1)} %collective-permute-done, bf16[3072,768]{1,0:T(8,128)(2,1)} %copy-done.1, s32[]{:T(128)S(6)} %select_n.31), kind=kLoop, calls=%fused_computation.9 | loop fusion | flops 4718592 | bytes 7077892 | tf_op jit(solution)/shard_map/convert_element_type | solution.py:46
  26.4 0.0 copy-start.3
  26.4 0.0 copy-start.4
  26.4 0.0 copy-start.5
  26.4 64.7 %all_to_all.20 = bf16[16,192,384]{2,1,0:T(8,128)(2,1)S(1)} all-to-all(bf16[16,192,384]{2,1,0:T(8,128)(2,1)S(1)} %bitcast.7), channel_id=1, replica_groups=mesh['shard'=16,'xl'=2,'z'=12,'c'=2] {'shard'}, dimensions={0} | all-to-all | bytes 4718592 | tf_op jit(solution)/shard_map/all_to_all | solution.py:45
  91.1 0.3 convert_reduce_fusion
  91.5 29.7 %all_to_all.21 = f32[24,8,384]{2,1,0:T(8,128)S(1)} all-to-all(f32[24,8,384]{2,1,0:T(8,128)S(1)} %bitcast.8), channel_id=1, replica_groups=mesh['shard'=16,'xl'=2,'z'=12,'c'=2] {'xl','z'}, dimensions={0} | all-to-all | bytes 589824 | tf_op jit(solution)/shard_map/all_to_all | solution.py:54
  121.3 15.8 %all_to_all.22 = f32[12,8,384]{2,1,0:T(8,128)S(1)} all-to-all(f32[12,8,384]{2,1,0:T(8,128)S(1)} %broadcast_in_dim.4), channel_id=1, replica_groups=mesh['shard'=16,'xl'=2,'z'=12,'c'=2] {'z'}, dimensions={0} | all-to-all | bytes 294912 | tf_op jit(solution)/shard_map/all_to_all | solution.py:57
  137.1 1.9 %collective-permute-start.1 = (f32[96,384]{1,0:T(8,128)S(1)}, f32[96,384]{1,0:T(8,128)S(1)}, u32[]{:S(2)}, u32[]{:S(2)}) collective-permute-start(f32[96,384]{1,0:T(8,128)S(1)} %bitcast.9), channel_id=1, source_target_pairs={{0,1},{1,0},{2,3},{3,2},{4,5},{5,4},{6,7},{7,6},{8,9},{9,8},{10,11... | collective-permute-start | bytes 442376 | tf_op jit(solution)/shard_map/ppermute | solution.py:59
  139.0 3.6 %collective-permute-start.2 = (f32[96,384]{1,0:T(8,128)S(1)}, f32[96,384]{1,0:T(8,128)S(1)}, u32[]{:S(2)}, u32[]{:S(2)}) collective-permute-start(f32[96,384]{1,0:T(8,128)S(1)} %bitcast.10), channel_id=1, source_target_pairs={{0,24},{24,0},{1,25},{25,1},{2,26},{26,2},{3,27},{27,3},{4,28},{28... | collective-permute-start | bytes 442376 | tf_op jit(solution)/shard_map/ppermute | solution.py:58
  142.6 2.1 %collective-permute-start.3 = (f32[96,384]{1,0:T(8,128)S(1)}, f32[96,384]{1,0:T(8,128)S(1)}, u32[]{:S(2)}, u32[]{:S(2)}) collective-permute-start(f32[96,384]{1,0:T(8,128)S(1)} %bitcast.11), channel_id=1, source_target_pairs={{0,25},{25,0},{1,24},{24,1},{2,27},{27,2},{3,26},{26,3},{4,29},{29... | collective-permute-start | bytes 442376 | tf_op jit(solution)/shard_map/ppermute | solution.py:60
  144.7 0.0 collective-permute-done.1
  144.8 2.4 %collective-permute-done.2 = f32[96,384]{1,0:T(8,128)S(1)} collective-permute-done((f32[96,384]{1,0:T(8,128)S(1)}, f32[96,384]{1,0:T(8,128)S(1)}, u32[]{:S(2)}, u32[]{:S(2)}) %collective-permute-start.2) | collective-permute-done | bytes 147488 | tf_op jit(solution)/shard_map/ppermute | solution.py:58
  147.2 3.1 %collective-permute-done.3 = f32[96,384]{1,0:T(8,128)S(1)} collective-permute-done((f32[96,384]{1,0:T(8,128)S(1)}, f32[96,384]{1,0:T(8,128)S(1)}, u32[]{:S(2)}, u32[]{:S(2)}) %collective-permute-start.3) | collective-permute-done | bytes 147488 | tf_op jit(solution)/shard_map/ppermute | solution.py:60
  150.3 0.0 copy-done.3
  150.3 0.0 copy-done.4
  150.3 0.0 copy-done.5
  150.3 1.5 multiply_subtract_fusion
  151.8 0.0 copy-start.2
  151.8 0.1 dynamic-slice_convert_fusion
  151.9 0.1 copy.23
  152.0 17.1 %all_to_all.23 = bf16[16,192,16]{1,2,0:T(8,128)(2,1)S(1)} all-to-all(bf16[16,192,16]{1,2,0:T(8,128)(2,1)S(1)} %broadcast_in_dim.5), channel_id=1, replica_groups=mesh['shard'=16,'xl'=2,'z'=12,'c'=2] {'shard'}, dimensions={0} | all-to-all | bytes 196608 | tf_op jit(solution)/shard_map/all_to_all | solution.py:75
  169.1 0.8 reshape.50
  169.9 0.0 copy-done.2
  (7 shorter events, 0.2 us)
Async XLA Ops:
  0.6 10.0 %copy-start = (bf16[2,196,768]{2,0,1:T(2,128)(2,1)S(1)}, bf16[2,196,768]{2,0,1:T(2,128)(2,1)}, u32[]{:S(2)}) copy-start(bf16[2,196,768]{2,0,1:T(2,128)(2,1)} %param.8) | copy-start | bytes 1806340
  13.6 2.1 %copy-start.1 = (bf16[3072,768]{1,0:T(8,128)(2,1)}, bf16[3072,768]{1,0:T(8,128)(2,1)S(1)}, u32[]{:S(2)}) copy-start(bf16[3072,768]{1,0:T(8,128)(2,1)S(1)} %bitcast_convert_fusion) | copy-start | bytes 14155780
  17.4 6.6 %collective-permute-start = (bf16[3072,384]{1,0:T(8,128)(2,1)}, bf16[3072,384]{1,0:T(8,128)(2,1)S(1)}, u32[]{:S(2)}, u32[]{:S(2)}) collective-permute-start(bf16[3072,384]{1,0:T(8,128)(2,1)} %constant_dynamic-slice_fusion), channel_id=1, source_target_pairs={{0,1},{1,0},{2,3},{3,2},{4,5},{5,4},{6,7},{7,6},{8,9},{9,8},{10,11... | collective-permute-start | bytes 7077896 | tf_op jit(solution)/shard_map/ppermute | solution.py:42
  26.4 123.9 %copy-start.3 = (f32[192,768]{1,0:T(8,128)S(1)}, f32[192,768]{1,0:T(8,128)}, u32[]{:S(2)}) copy-start(f32[192,768]{1,0:T(8,128)} %param.11) | copy-start | bytes 1769476
  26.4 123.9 %copy-start.4 = (f32[192,768]{1,0:T(8,128)S(1)}, f32[192,768]{1,0:T(8,128)}, u32[]{:S(2)}) copy-start(f32[192,768]{1,0:T(8,128)} %param.12) | copy-start | bytes 1769476
  26.4 123.9 %copy-start.5 = (f32[192,768]{1,0:T(8,128)S(1)}, f32[192,768]{1,0:T(8,128)}, u32[]{:S(2)}) copy-start(f32[192,768]{1,0:T(8,128)} %param.13) | copy-start | bytes 1769476
  137.1 7.6 %collective-permute-start.1 = (f32[96,384]{1,0:T(8,128)S(1)}, f32[96,384]{1,0:T(8,128)S(1)}, u32[]{:S(2)}, u32[]{:S(2)}) collective-permute-start(f32[96,384]{1,0:T(8,128)S(1)} %bitcast.9), channel_id=1, source_target_pairs={{0,1},{1,0},{2,3},{3,2},{4,5},{5,4},{6,7},{7,6},{8,9},{9,8},{10,11... | collective-permute-start | bytes 442376 | tf_op jit(solution)/shard_map/ppermute | solution.py:59
  139.0 8.1 %collective-permute-start.2 = (f32[96,384]{1,0:T(8,128)S(1)}, f32[96,384]{1,0:T(8,128)S(1)}, u32[]{:S(2)}, u32[]{:S(2)}) collective-permute-start(f32[96,384]{1,0:T(8,128)S(1)} %bitcast.10), channel_id=1, source_target_pairs={{0,24},{24,0},{1,25},{25,1},{2,26},{26,2},{3,27},{27,3},{4,28},{28... | collective-permute-start | bytes 442376 | tf_op jit(solution)/shard_map/ppermute | solution.py:58
  142.6 7.6 %collective-permute-start.3 = (f32[96,384]{1,0:T(8,128)S(1)}, f32[96,384]{1,0:T(8,128)S(1)}, u32[]{:S(2)}, u32[]{:S(2)}) collective-permute-start(f32[96,384]{1,0:T(8,128)S(1)} %bitcast.11), channel_id=1, source_target_pairs={{0,25},{25,0},{1,24},{24,1},{2,27},{27,2},{3,26},{26,3},{4,29},{29... | collective-permute-start | bytes 442376 | tf_op jit(solution)/shard_map/ppermute | solution.py:60
  151.8 18.2 %copy-start.2 = (f32[192,768]{1,0:T(8,128)}, f32[192,768]{1,0:T(8,128)S(1)}, u32[]{:S(2)}) copy-start(f32[192,768]{1,0:T(8,128)S(1)} %get-tuple-element.4) | copy-start | bytes 1769476

commit v5 on v4

--- a/solution.py
+++ b/solution.py
@@ -51,8 +51,10 @@
     n_z = lax.axis_size("z")
     n_xz = lax.axis_size(("xl", "z"))
     sub = block // n_xz
-    pieces2 = lax.all_to_all(part.reshape(n_xz, sub, half), ("xl", "z"), 0, 0, tiled=True)
-    grad_sub = jnp.sum(pieces2, axis=0)
+    pieces2 = lax.all_to_all(
+        part.astype(jnp.bfloat16).reshape(n_xz, sub, half), ("xl", "z"), 0, 0, tiled=True
+    )
+    grad_sub = jnp.sum(pieces2.astype(jnp.float32), axis=0)
     spread = jnp.broadcast_to(grad_sub[None], (n_z, sub, half))
     grad_quarter = lax.all_to_all(spread, "z", 0, 0, tiled=True).reshape(rows_half, half)
     from_x = lax.ppermute(grad_quarter, "xl", SWAP)

time: 172 us -> 170 us (0.988)
  blocking collectives: 127 us -> 123 us
  other arithmetic: 14.2 us -> 16.1 us
    all_to_all x1, blocking collectives: 29.7 us -> 27.5 us  [body(): lax.all_to_all(part.astype(jnp.bfloat16).reshape(n_xz, sub, half), ('xl',...]
where the time goes in v5:
time: 170 us; the launch traced here: 167 us
  blocking collectives  123 us (72%)
  other arithmetic  16.1 us (9%)
  waiting for transfers between devices  10.1 us (6%)
  starting transfers between devices  9.48 us (6%)
  local copies, waits for them, and re-layouts  4.85 us (3%)
  matrix products  3 us (2%)
    all_to_all x1, blocking collectives, body(): lax.all_to_all(chip.astype(jnp.bfloat16).reshape(n_shard, block, half), '...  64.7 us
    all_to_all x1, blocking collectives, body(): lax.all_to_all(part.astype(jnp.bfloat16).reshape(n_xz, sub, half), ('xl',...  27.5 us
    all_to_all x1, blocking collectives, body(): lax.all_to_all(spread_cols, 'shard', 0, 0, tiled=True)  15.4 us
    all_to_all x1, blocking collectives, body(): lax.all_to_all(spread, 'z', 0, 0, tiled=True).reshape(rows_half, half)  15.1 us
    convert_element_type x1, other arithmetic, grn_forward(): return grn_out.astype(jnp.bfloat16)  5.42 us
    ppermute x1, waiting for transfers between devices, body(): lax.ppermute(other, 'c', SWAP).astype(jnp.float32)  4.71 us
    reduce_sum x1, other arithmetic, grn_forward(): spatial_norm = jnp.sqrt(jnp.sum(values * values, axis=1))  4.29 us
    ppermute x1, starting transfers between devices, body(): from_x = lax.ppermute(grad_quarter, 'xl', SWAP)  3.45 us
  transfers between devices with their start and end apart: 4, of which 3 were waited for; matrix products, arithmetic and copies ran while one was open for 0% of the time, Pallas kernels for 0%

profile of v5, /device:TPU:6, one launch (start us, length us, event | category | flops | bytes accessed | tf_op | source)
XLA Modules:
  0.0 167.1 jit_solution(14778852932415800025)
XLA Ops:
  0.6 0.0 copy-start
  0.7 4.3 %fusion = f32[2,3072]{1,0:T(2,128)S(1)} fusion(bf16[2,196,3072]{2,0,1:T(2,128)(2,1)} %param.7), kind=kLoop, calls=%fused_computation.4 | loop fusion | flops 3606528 | bytes 2433024 | tf_op jit(solution)/shard_map/reduce_sum | solution.py:20
  4.9 0.1 sqrt_reduce_fusion
  5.1 0.1 sqrt_divide_fusion
  5.2 5.4 %fusion.3 = bf16[2,196,3072]{2,0,1:T(2,128)(2,1)S(1)} fusion(bf16[2,196,3072]{2,0,1:T(2,128)(2,1)} %param.7, f32[3072]{0:T(1024)} %param.10, f32[2,3072]{1,0:T(2,128)S(1)} %sqrt_divide_fusion, f32[3072]{0:T(1024)} %param.9), kind=kLoop, calls=%fused_computation.7 | loop fusion | flops 7225344 | bytes 4866048 | tf_op jit(solution)/shard_map/convert_element_type | solution.py:23
  10.6 0.0 copy-done
  10.6 3.0 %bitcast_convert_fusion = bf16[3072,768]{1,0:T(8,128)(2,1)S(1)} fusion(bf16[2,196,3072]{2,0,1:T(2,128)(2,1)S(1)} %fusion.3, bf16[2,196,768]{2,0,1:T(2,128)(2,1)S(1)} %copy-done), kind=kOutput, calls=%fused_computation | convolution fusion | flops 1852047360 | bytes 7729152 | tf_op jit(solution)/shard_map/dot_general | solution.py:35
  13.6 0.0 copy-start.1
  13.6 2.1 %copy-done.1 = bf16[3072,768]{1,0:T(8,128)(2,1)} copy-done((bf16[3072,768]{1,0:T(8,128)(2,1)}, bf16[3072,768]{1,0:T(8,128)(2,1)S(1)}, u32[]{:S(2)}) %copy-start.1) | copy-done | bytes 4718616
  15.7 1.7 %constant_dynamic-slice_fusion = bf16[3072,384]{1,0:T(8,128)(2,1)} fusion(bf16[3072,768]{1,0:T(8,128)(2,1)S(1)} %bitcast_convert_fusion, s32[]{:T(128)S(6)} %select_n.32), kind=kLoop, calls=%fused_computation.22 | loop fusion | bytes 4718596 | tf_op jit(solution)/shard_map/dynamic_slice | solution.py:41
  17.4 1.9 %collective-permute-start = (bf16[3072,384]{1,0:T(8,128)(2,1)}, bf16[3072,384]{1,0:T(8,128)(2,1)S(1)}, u32[]{:S(2)}, u32[]{:S(2)}) collective-permute-start(bf16[3072,384]{1,0:T(8,128)(2,1)} %constant_dynamic-slice_fusion), channel_id=1, source_target_pairs={{0,1},{1,0},{2,3},{3,2},{4,5},{5,4},{6,7},{7,6},{8,9},{9,8},{10,11... | collective-permute-start | bytes 7077896 | tf_op jit(solution)/shard_map/ppermute | solution.py:42
  19.3 4.7 %collective-permute-done = bf16[3072,384]{1,0:T(8,128)(2,1)S(1)} collective-permute-done((bf16[3072,384]{1,0:T(8,128)(2,1)}, bf16[3072,384]{1,0:T(8,128)(2,1)S(1)}, u32[]{:S(2)}, u32[]{:S(2)}) %collective-permute-start) | collective-permute-done | bytes 2359328 | tf_op jit(solution)/shard_map/ppermute | solution.py:42
  24.1 2.3 %add_convert_fusion = bf16[3072,384]{1,0:T(8,128)(2,1)S(1)} fusion(bf16[3072,384]{1,0:T(8,128)(2,1)S(1)} %collective-permute-done, bf16[3072,768]{1,0:T(8,128)(2,1)} %copy-done.1, s32[]{:T(128)S(6)} %select_n.31), kind=kLoop, calls=%fused_computation.8 | loop fusion | flops 4718592 | bytes 7077892 | tf_op jit(solution)/shard_map/convert_element_type | solution.py:46
  26.4 0.0 copy-start.3
  26.4 64.7 %all_to_all.20 = bf16[16,192,384]{2,1,0:T(8,128)(2,1)S(1)} all-to-all(bf16[16,192,384]{2,1,0:T(8,128)(2,1)S(1)} %bitcast.7), channel_id=1, replica_groups=mesh['shard'=16,'xl'=2,'z'=12,'c'=2] {'shard'}, dimensions={0} | all-to-all | bytes 4718592 | tf_op jit(solution)/shard_map/all_to_all | solution.py:45
  91.1 1.0 reduce_sum.41
  92.1 27.5 %all_to_all.21 = bf16[24,8,384]{2,1,0:T(8,128)(2,1)S(1)} all-to-all(bf16[24,8,384]{2,1,0:T(8,128)(2,1)} %bitcast.12), channel_id=1, replica_groups=mesh['shard'=16,'xl'=2,'z'=12,'c'=2] {'xl','z'}, dimensions={0} | all-to-all | bytes 294912 | tf_op jit(solution)/shard_map/all_to_all | solution.py:54
  119.7 15.1 %all_to_all.22 = f32[12,8,384]{2,1,0:T(8,128)S(1)} all-to-all(f32[12,8,384]{2,1,0:T(8,128)S(1)} %broadcast_in_dim.4), channel_id=1, replica_groups=mesh['shard'=16,'xl'=2,'z'=12,'c'=2] {'z'}, dimensions={0} | all-to-all | bytes 294912 | tf_op jit(solution)/shard_map/all_to_all | solution.py:59
  134.8 1.9 %collective-permute-start.1 = (f32[96,384]{1,0:T(8,128)S(1)}, f32[96,384]{1,0:T(8,128)S(1)}, u32[]{:S(2)}, u32[]{:S(2)}) collective-permute-start(f32[96,384]{1,0:T(8,128)S(1)} %bitcast.8), channel_id=1, source_target_pairs={{0,1},{1,0},{2,3},{3,2},{4,5},{5,4},{6,7},{7,6},{8,9},{9,8},{10,11... | collective-permute-start | bytes 442376 | tf_op jit(solution)/shard_map/ppermute | solution.py:61
  136.7 3.4 %collective-permute-start.2 = (f32[96,384]{1,0:T(8,128)S(1)}, f32[96,384]{1,0:T(8,128)S(1)}, u32[]{:S(2)}, u32[]{:S(2)}) collective-permute-start(f32[96,384]{1,0:T(8,128)S(1)} %bitcast.9), channel_id=1, source_target_pairs={{0,24},{24,0},{1,25},{25,1},{2,26},{26,2},{3,27},{27,3},{4,28},{28... | collective-permute-start | bytes 442376 | tf_op jit(solution)/shard_map/ppermute | solution.py:60
  140.1 2.2 %collective-permute-start.3 = (f32[96,384]{1,0:T(8,128)S(1)}, f32[96,384]{1,0:T(8,128)S(1)}, u32[]{:S(2)}, u32[]{:S(2)}) collective-permute-start(f32[96,384]{1,0:T(8,128)S(1)} %bitcast.10), channel_id=1, source_target_pairs={{0,25},{25,0},{1,24},{24,1},{2,27},{27,2},{3,26},{26,3},{4,29},{29... | collective-permute-start | bytes 442376 | tf_op jit(solution)/shard_map/ppermute | solution.py:62
  142.4 0.0 collective-permute-done.1
  142.4 2.4 %collective-permute-done.2 = f32[96,384]{1,0:T(8,128)S(1)} collective-permute-done((f32[96,384]{1,0:T(8,128)S(1)}, f32[96,384]{1,0:T(8,128)S(1)}, u32[]{:S(2)}, u32[]{:S(2)}) %collective-permute-start.2) | collective-permute-done | bytes 147488 | tf_op jit(solution)/shard_map/ppermute | solution.py:60
  144.8 3.0 %collective-permute-done.3 = f32[96,384]{1,0:T(8,128)S(1)} collective-permute-done((f32[96,384]{1,0:T(8,128)S(1)}, f32[96,384]{1,0:T(8,128)S(1)}, u32[]{:S(2)}, u32[]{:S(2)}) %collective-permute-start.3) | collective-permute-done | bytes 147488 | tf_op jit(solution)/shard_map/ppermute | solution.py:62
  147.8 0.0 copy-done.3
  147.8 2.7 %multiply_subtract_fusion = (f32[192,768]{1,0:T(8,128)S(1)}, f32[192,768]{1,0:T(8,128)}, f32[192,768]{1,0:T(8,128)}) fusion(f32[192,768]{1,0:T(8,128)S(1)} %copy-done.3, f32[96,768]{1,0:T(8,128)S(1)} %maximum_select_fusion.1, f32[96,768]{1,0:T(8,128)S(1)} %maximum_select_fusion.2, pred[]{:T(512)S(6)} %eq.7, f32[192,768]{1,0:T(8,128)} %param.12, ...), kind=kLoop, calls=%fused_computation.14 | loop fusion | flops 2654208 | bytes 4128769 | tf_op jit(solution)/shard_map/sub | solution.py:71
  150.6 0.0 copy-start.2
  150.6 0.1 dynamic-slice_convert_fusion
  150.7 0.1 copy.23
  150.8 15.4 %all_to_all.23 = bf16[16,192,16]{1,2,0:T(8,128)(2,1)S(1)} all-to-all(bf16[16,192,16]{1,2,0:T(8,128)(2,1)S(1)} %broadcast_in_dim.5), channel_id=1, replica_groups=mesh['shard'=16,'xl'=2,'z'=12,'c'=2] {'shard'}, dimensions={0} | all-to-all | bytes 196608 | tf_op jit(solution)/shard_map/all_to_all | solution.py:77
  166.2 0.8 reshape.50
  167.1 0.0 copy-done.2
  (7 shorter events, 0.2 us)
Async XLA Ops:
  0.6 10.0 %copy-start = (bf16[2,196,768]{2,0,1:T(2,128)(2,1)S(1)}, bf16[2,196,768]{2,0,1:T(2,128)(2,1)}, u32[]{:S(2)}) copy-start(bf16[2,196,768]{2,0,1:T(2,128)(2,1)} %param.8) | copy-start | bytes 1806340
  13.6 2.1 %copy-start.1 = (bf16[3072,768]{1,0:T(8,128)(2,1)}, bf16[3072,768]{1,0:T(8,128)(2,1)S(1)}, u32[]{:S(2)}) copy-start(bf16[3072,768]{1,0:T(8,128)(2,1)S(1)} %bitcast_convert_fusion) | copy-start | bytes 14155780
  17.4 6.6 %collective-permute-start = (bf16[3072,384]{1,0:T(8,128)(2,1)}, bf16[3072,384]{1,0:T(8,128)(2,1)S(1)}, u32[]{:S(2)}, u32[]{:S(2)}) collective-permute-start(bf16[3072,384]{1,0:T(8,128)(2,1)} %constant_dynamic-slice_fusion), channel_id=1, source_target_pairs={{0,1},{1,0},{2,3},{3,2},{4,5},{5,4},{6,7},{7,6},{8,9},{9,8},{10,11... | collective-permute-start | bytes 7077896 | tf_op jit(solution)/shard_map/ppermute | solution.py:42
  26.4 121.4 %copy-start.3 = (f32[192,768]{1,0:T(8,128)S(1)}, f32[192,768]{1,0:T(8,128)}, u32[]{:S(2)}) copy-start(f32[192,768]{1,0:T(8,128)} %param.11) | copy-start | bytes 1769476
  134.8 7.6 %collective-permute-start.1 = (f32[96,384]{1,0:T(8,128)S(1)}, f32[96,384]{1,0:T(8,128)S(1)}, u32[]{:S(2)}, u32[]{:S(2)}) collective-permute-start(f32[96,384]{1,0:T(8,128)S(1)} %bitcast.8), channel_id=1, source_target_pairs={{0,1},{1,0},{2,3},{3,2},{4,5},{5,4},{6,7},{7,6},{8,9},{9,8},{10,11... | collective-permute-start | bytes 442376 | tf_op jit(solution)/shard_map/ppermute | solution.py:61
  136.7 8.1 %collective-permute-start.2 = (f32[96,384]{1,0:T(8,128)S(1)}, f32[96,384]{1,0:T(8,128)S(1)}, u32[]{:S(2)}, u32[]{:S(2)}) collective-permute-start(f32[96,384]{1,0:T(8,128)S(1)} %bitcast.9), channel_id=1, source_target_pairs={{0,24},{24,0},{1,25},{25,1},{2,26},{26,2},{3,27},{27,3},{4,28},{28... | collective-permute-start | bytes 442376 | tf_op jit(solution)/shard_map/ppermute | solution.py:60
  140.1 7.6 %collective-permute-start.3 = (f32[96,384]{1,0:T(8,128)S(1)}, f32[96,384]{1,0:T(8,128)S(1)}, u32[]{:S(2)}, u32[]{:S(2)}) collective-permute-start(f32[96,384]{1,0:T(8,128)S(1)} %bitcast.10), channel_id=1, source_target_pairs={{0,25},{25,0},{1,24},{24,1},{2,27},{27,2},{3,26},{26,3},{4,29},{29... | collective-permute-start | bytes 442376 | tf_op jit(solution)/shard_map/ppermute | solution.py:62
  150.6 16.5 %copy-start.2 = (f32[192,768]{1,0:T(8,128)}, f32[192,768]{1,0:T(8,128)S(1)}, u32[]{:S(2)}) copy-start(f32[192,768]{1,0:T(8,128)S(1)} %get-tuple-element.4) | copy-start | bytes 1769476

commit v6 on v5

--- a/solution.py
+++ b/solution.py
@@ -30,10 +30,12 @@
 def body(hidden_act, out_grad, grn_gamma, grn_beta, master, moment_one, moment_two):
     images, positions, hidden = hidden_act.shape
     channels = out_grad.shape[2]
-    flat_rows = grn_forward(hidden_act, grn_gamma, grn_beta).reshape(images * positions, hidden)
-    flat_grads = out_grad.reshape(images * positions, channels)
-    term = lax.dot_general(
-        flat_rows, flat_grads, (((0,), (0,)), ((), ())), preferred_element_type=jnp.float32
+    grn_out = grn_forward(hidden_act, grn_gamma, grn_beta)
+    term = sum(
+        lax.dot_general(
+            grn_out[i], out_grad[i], (((0,), (0,)), ((), ())), preferred_element_type=jnp.float32
+        )
+        for i in range(images)
     ).astype(jnp.bfloat16)
     core = lax.axis_index("c")
     half = channels // CORES

time: 170 us -> 166 us (0.976)
  other arithmetic: 16.1 us -> 8.51 us
  matrix products: 3 us -> 5.17 us
    convert_element_type x1, other arithmetic: 5.42 us -> 0.99 us  [grn_forward(): return grn_out.astype(jnp.bfloat16)]
    dot_general x1 -> x2, matrix products: 3 us -> 5.17 us  [body(): lax.dot_general(grn_out[i], out_grad[i], (((0,), (0,)), ((), ())), prefer...]
    unnamed x8 -> x18, local copies, waits for them, and re-layouts: 2.14 us -> 0.11 us
    reduce_sum x1, other arithmetic: 4.29 us -> 2.46 us  [grn_forward(): spatial_norm = jnp.sqrt(jnp.sum(values * values, axis=1))]
where the time goes in v6:
time: 166 us; the launch traced here: 163 us
  blocking collectives  123 us (74%)
  waiting for transfers between devices  9.9 us (6%)
  starting transfers between devices  9.76 us (6%)
  other arithmetic  8.51 us (5%)
  local copies, waits for them, and re-layouts  6.13 us (4%)
  matrix products  5.17 us (3%)
    all_to_all x1, blocking collectives, body(): lax.all_to_all(chip.astype(jnp.bfloat16).reshape(n_shard, block, half), '...  64.6 us
    all_to_all x1, blocking collectives, body(): lax.all_to_all(part.astype(jnp.bfloat16).reshape(n_xz, sub, half), ('xl',...  27.6 us
    all_to_all x1, blocking collectives, body(): lax.all_to_all(spread_cols, 'shard', 0, 0, tiled=True)  15.2 us
    all_to_all x1, blocking collectives, body(): lax.all_to_all(spread, 'z', 0, 0, tiled=True).reshape(rows_half, half)  15.1 us
    dot_general x2, matrix products, body(): lax.dot_general(grn_out[i], out_grad[i], (((0,), (0,)), ((), ())), prefer...  5.17 us
    ppermute x1, waiting for transfers between devices, body(): lax.ppermute(other, 'c', SWAP).astype(jnp.float32)  4.71 us
    ppermute x1, starting transfers between devices, body(): lax.ppermute(grad_quarter, ('xl', 'c'), [(0, 3), (3, 0), (1, 2), (2, 1)])  3.55 us
    ppermute x1, waiting for transfers between devices, body(): from_x = lax.ppermute(grad_quarter, 'xl', SWAP)  3.44 us
  transfers between devices with their start and end apart: 4, of which 3 were waited for; matrix products, arithmetic and copies ran while one was open for 0% of the time, Pallas kernels for 0%

profile of v6, /device:TPU:6, one launch (start us, length us, event | category | flops | bytes accessed | tf_op | source)
XLA Modules:
  0.0 162.8 jit_solution(16919437586263564458)
XLA Ops:
  0.6 0.0 copy-start.1
  0.6 0.0 copy-start
  0.7 0.0 copy-start.7
  0.7 0.0 copy-start.8
  0.7 2.5 %fusion = f32[2,3072]{1,0:T(2,128)S(1)} fusion(bf16[2,196,3072]{2,0,1:T(2,128)(2,1)} %param.7), kind=kLoop, calls=%fused_computation.4 | loop fusion | flops 3606528 | bytes 2433024 | tf_op jit(solution)/shard_map/reduce_sum | solution.py:20
  3.1 0.1 sqrt_reduce_fusion
  3.3 0.1 sqrt_divide_fusion
  3.4 0.0 copy-done.1
  3.4 1.7 %fusion.7 = (bf16[1,196,768]{2,0,1:T(2,128)(2,1)S(1)}, bf16[1,196,768]{2,0,1:T(2,128)(2,1)}) fusion(bf16[2,196,768]{2,0,1:T(2,128)(2,1)S(1)} %copy-done.1), kind=kLoop, calls=%fused_computation.27 | loop fusion | bytes 1204224 | tf_op jit(solution)/shard_map/slice | solution.py:36
  5.0 0.0 copy-done
  5.0 0.0 copy-done.7
  5.0 0.0 copy-done.8
  5.0 0.0 copy-start.2
  5.0 1.0 fusion.3
  6.0 0.1 copy-done.2
  6.1 1.5 fusion.4
  7.6 3.7 %add_convert_fusion = bf16[3072,768]{1,0:T(8,128)(2,1)} fusion(f32[3072,768]{1,0:T(8,128)S(1)} %fusion.4, bf16[2,196,3072]{2,1,0:T(8,128)(2,1)S(1)} %fusion.3, bf16[1,196,768]{2,0,1:T(2,128)(2,1)S(1)} %get-tuple-element.7), kind=kOutput, calls=%fused_computation | convolution fusion | flops 929562624 | bytes 15986688 | tf_op jit(solution)/shard_map/dot_general | solution.py:35
  11.3 3.3 %constant_dynamic-slice_fusion = bf16[3072,384]{1,0:T(8,128)(2,1)} fusion(bf16[3072,768]{1,0:T(8,128)(2,1)} %add_convert_fusion, s32[]{:T(128)S(6)} %select_n.32), kind=kLoop, calls=%fused_computation.25 | loop fusion | bytes 4718596 | tf_op jit(solution)/shard_map/dynamic_slice | solution.py:43
  14.6 1.9 %collective-permute-start = (bf16[3072,384]{1,0:T(8,128)(2,1)}, bf16[3072,384]{1,0:T(8,128)(2,1)S(1)}, u32[]{:S(2)}, u32[]{:S(2)}) collective-permute-start(bf16[3072,384]{1,0:T(8,128)(2,1)} %constant_dynamic-slice_fusion), channel_id=1, source_target_pairs={{0,1},{1,0},{2,3},{3,2},{4,5},{5,4},{6,7},{7,6},{8,9},{9,8},{10,11... | collective-permute-start | bytes 7077896 | tf_op jit(solution)/shard_map/ppermute | solution.py:44
  16.6 4.7 %collective-permute-done = bf16[3072,384]{1,0:T(8,128)(2,1)S(1)} collective-permute-done((bf16[3072,384]{1,0:T(8,128)(2,1)}, bf16[3072,384]{1,0:T(8,128)(2,1)S(1)}, u32[]{:S(2)}, u32[]{:S(2)}) %collective-permute-start) | collective-permute-done | bytes 2359328 | tf_op jit(solution)/shard_map/ppermute | solution.py:44
  21.3 2.3 %add_convert_fusion.1 = bf16[3072,384]{1,0:T(8,128)(2,1)S(1)} fusion(bf16[3072,384]{1,0:T(8,128)(2,1)S(1)} %collective-permute-done, bf16[3072,768]{1,0:T(8,128)(2,1)} %add_convert_fusion, s32[]{:T(128)S(6)} %select_n.31), kind=kLoop, calls=%fused_computation.8 | loop fusion | flops 4718592 | bytes 7077892 | tf_op jit(solution)/shard_map/convert_element_type | solution.py:48
  23.5 64.6 %all_to_all.20 = bf16[16,192,384]{2,1,0:T(8,128)(2,1)S(1)} all-to-all(bf16[16,192,384]{2,1,0:T(8,128)(2,1)S(1)} %bitcast.17), channel_id=1, replica_groups=mesh['shard'=16,'xl'=2,'z'=12,'c'=2] {'shard'}, dimensions={0} | all-to-all | bytes 4718592 | tf_op jit(solution)/shard_map/all_to_all | solution.py:47
  88.1 0.0 copy-start.4
  88.1 0.0 copy-start.5
  88.1 1.0 reduce_sum.41
  89.1 0.0 copy-start.6
  89.1 27.6 %all_to_all.21 = bf16[24,8,384]{2,1,0:T(8,128)(2,1)S(1)} all-to-all(bf16[24,8,384]{2,1,0:T(8,128)(2,1)} %bitcast.22), channel_id=1, replica_groups=mesh['shard'=16,'xl'=2,'z'=12,'c'=2] {'xl','z'}, dimensions={0} | all-to-all | bytes 294912 | tf_op jit(solution)/shard_map/all_to_all | solution.py:56
  116.8 15.1 %all_to_all.22 = f32[12,8,384]{2,1,0:T(8,128)S(1)} all-to-all(f32[12,8,384]{2,1,0:T(8,128)S(1)} %broadcast_in_dim.4), channel_id=1, replica_groups=mesh['shard'=16,'xl'=2,'z'=12,'c'=2] {'z'}, dimensions={0} | all-to-all | bytes 294912 | tf_op jit(solution)/shard_map/all_to_all | solution.py:61
  131.9 1.9 %collective-permute-start.1 = (f32[96,384]{1,0:T(8,128)S(1)}, f32[96,384]{1,0:T(8,128)S(1)}, u32[]{:S(2)}, u32[]{:S(2)}) collective-permute-start(f32[96,384]{1,0:T(8,128)S(1)} %bitcast.18), channel_id=1, source_target_pairs={{0,1},{1,0},{2,3},{3,2},{4,5},{5,4},{6,7},{7,6},{8,9},{9,8},{10,11... | collective-permute-start | bytes 442376 | tf_op jit(solution)/shard_map/ppermute | solution.py:63
  133.8 3.5 %collective-permute-start.3 = (f32[96,384]{1,0:T(8,128)S(1)}, f32[96,384]{1,0:T(8,128)S(1)}, u32[]{:S(2)}, u32[]{:S(2)}) collective-permute-start(f32[96,384]{1,0:T(8,128)S(1)} %bitcast.19), channel_id=1, source_target_pairs={{0,25},{25,0},{1,24},{24,1},{2,27},{27,2},{3,26},{26,3},{4,29},{29... | collective-permute-start | bytes 442376 | tf_op jit(solution)/shard_map/ppermute | solution.py:64
  137.4 2.4 %collective-permute-start.2 = (f32[96,384]{1,0:T(8,128)S(1)}, f32[96,384]{1,0:T(8,128)S(1)}, u32[]{:S(2)}, u32[]{:S(2)}) collective-permute-start(f32[96,384]{1,0:T(8,128)S(1)} %bitcast.20), channel_id=1, source_target_pairs={{0,24},{24,0},{1,25},{25,1},{2,26},{26,2},{3,27},{27,3},{4,28},{28... | collective-permute-start | bytes 442376 | tf_op jit(solution)/shard_map/ppermute | solution.py:62
  139.8 0.0 collective-permute-done.1
  139.8 1.7 %collective-permute-done.3 = f32[96,384]{1,0:T(8,128)S(1)} collective-permute-done((f32[96,384]{1,0:T(8,128)S(1)}, f32[96,384]{1,0:T(8,128)S(1)}, u32[]{:S(2)}, u32[]{:S(2)}) %collective-permute-start.3) | collective-permute-done | bytes 147488 | tf_op jit(solution)/shard_map/ppermute | solution.py:64
  141.6 3.4 %collective-permute-done.2 = f32[96,384]{1,0:T(8,128)S(1)} collective-permute-done((f32[96,384]{1,0:T(8,128)S(1)}, f32[96,384]{1,0:T(8,128)S(1)}, u32[]{:S(2)}, u32[]{:S(2)}) %collective-permute-start.2) | collective-permute-done | bytes 147488 | tf_op jit(solution)/shard_map/ppermute | solution.py:62
  145.1 0.0 copy-done.4
  145.1 0.0 copy-done.5
  145.1 0.0 copy-done.6
  145.1 1.5 multiply_subtract_fusion
  146.6 0.0 copy-start.3
  146.6 0.1 dynamic-slice_convert_fusion
  146.7 0.1 copy.28
  146.8 15.2 %all_to_all.23 = bf16[16,192,16]{1,2,0:T(8,128)(2,1)S(1)} all-to-all(bf16[16,192,16]{1,2,0:T(8,128)(2,1)S(1)} %broadcast_in_dim.5), channel_id=1, replica_groups=mesh['shard'=16,'xl'=2,'z'=12,'c'=2] {'shard'}, dimensions={0} | all-to-all | bytes 196608 | tf_op jit(solution)/shard_map/all_to_all | solution.py:79
  162.0 0.8 reshape.48
  162.8 0.0 copy-done.3
  (7 shorter events, 0.2 us)
Async XLA Ops:
  0.6 2.7 %copy-start.1 = (bf16[2,196,768]{2,0,1:T(2,128)(2,1)S(1)}, bf16[2,196,768]{2,0,1:T(2,128)(2,1)}, u32[]{:S(2)}) copy-start(bf16[2,196,768]{2,0,1:T(2,128)(2,1)} %param.8) | copy-start | bytes 1806340
  0.6 4.4 %copy-start = (bf16[2,196,3072]{2,0,1:T(2,128)(2,1)S(1)}, bf16[2,196,3072]{2,0,1:T(2,128)(2,1)}, u32[]{:S(2)}) copy-start(bf16[2,196,3072]{2,0,1:T(2,128)(2,1)} %param.7) | copy-start | bytes 7225348
  0.7 4.4 %copy-start.7 = (f32[3072]{0:T(1024)S(1)}, f32[3072]{0:T(1024)}, u32[]{:S(2)}) copy-start(f32[3072]{0:T(1024)} %param.10) | copy-start | bytes 36868
  0.7 4.4 %copy-start.8 = (f32[3072]{0:T(1024)S(1)}, f32[3072]{0:T(1024)}, u32[]{:S(2)}) copy-start(f32[3072]{0:T(1024)} %param.9) | copy-start | bytes 36868
  5.0 1.1 copy-start.2
  14.6 6.6 %collective-permute-start = (bf16[3072,384]{1,0:T(8,128)(2,1)}, bf16[3072,384]{1,0:T(8,128)(2,1)S(1)}, u32[]{:S(2)}, u32[]{:S(2)}) collective-permute-start(bf16[3072,384]{1,0:T(8,128)(2,1)} %constant_dynamic-slice_fusion), channel_id=1, source_target_pairs={{0,1},{1,0},{2,3},{3,2},{4,5},{5,4},{6,7},{7,6},{8,9},{9,8},{10,11... | collective-permute-start | bytes 7077896 | tf_op jit(solution)/shard_map/ppermute | solution.py:44
  88.1 57.0 %copy-start.4 = (f32[192,768]{1,0:T(8,128)S(1)}, f32[192,768]{1,0:T(8,128)}, u32[]{:S(2)}) copy-start(f32[192,768]{1,0:T(8,128)} %param.11) | copy-start | bytes 1769476
  88.1 57.0 %copy-start.5 = (f32[192,768]{1,0:T(8,128)S(1)}, f32[192,768]{1,0:T(8,128)}, u32[]{:S(2)}) copy-start(f32[192,768]{1,0:T(8,128)} %param.12) | copy-start | bytes 1769476
  89.1 56.0 %copy-start.6 = (f32[192,768]{1,0:T(8,128)S(1)}, f32[192,768]{1,0:T(8,128)}, u32[]{:S(2)}) copy-start(f32[192,768]{1,0:T(8,128)} %param.13) | copy-start | bytes 1769476
  131.9 7.9 %collective-permute-start.1 = (f32[96,384]{1,0:T(8,128)S(1)}, f32[96,384]{1,0:T(8,128)S(1)}, u32[]{:S(2)}, u32[]{:S(2)}) collective-permute-start(f32[96,384]{1,0:T(8,128)S(1)} %bitcast.18), channel_id=1, source_target_pairs={{0,1},{1,0},{2,3},{3,2},{4,5},{5,4},{6,7},{7,6},{8,9},{9,8},{10,11... | collective-permute-start | bytes 442376 | tf_op jit(solution)/shard_map/ppermute | solution.py:63
  133.8 7.8 %collective-permute-start.3 = (f32[96,384]{1,0:T(8,128)S(1)}, f32[96,384]{1,0:T(8,128)S(1)}, u32[]{:S(2)}, u32[]{:S(2)}) collective-permute-start(f32[96,384]{1,0:T(8,128)S(1)} %bitcast.19), channel_id=1, source_target_pairs={{0,25},{25,0},{1,24},{24,1},{2,27},{27,2},{3,26},{26,3},{4,29},{29... | collective-permute-start | bytes 442376 | tf_op jit(solution)/shard_map/ppermute | solution.py:64
  137.4 7.7 %collective-permute-start.2 = (f32[96,384]{1,0:T(8,128)S(1)}, f32[96,384]{1,0:T(8,128)S(1)}, u32[]{:S(2)}, u32[]{:S(2)}) collective-permute-start(f32[96,384]{1,0:T(8,128)S(1)} %bitcast.20), channel_id=1, source_target_pairs={{0,24},{24,0},{1,25},{25,1},{2,26},{26,2},{3,27},{27,3},{4,28},{28... | collective-permute-start | bytes 442376 | tf_op jit(solution)/shard_map/ppermute | solution.py:62
  146.6 16.2 %copy-start.3 = (f32[192,768]{1,0:T(8,128)}, f32[192,768]{1,0:T(8,128)S(1)}, u32[]{:S(2)}) copy-start(f32[192,768]{1,0:T(8,128)S(1)} %get-tuple-element.4) | copy-start | bytes 1769476

commit v7 on v6

--- a/solution.py
+++ b/solution.py
@@ -31,17 +31,20 @@
     images, positions, hidden = hidden_act.shape
     channels = out_grad.shape[2]
     grn_out = grn_forward(hidden_act, grn_gamma, grn_beta)
-    term = sum(
-        lax.dot_general(
-            grn_out[i], out_grad[i], (((0,), (0,)), ((), ())), preferred_element_type=jnp.float32
-        )
-        for i in range(images)
-    ).astype(jnp.bfloat16)
     core = lax.axis_index("c")
     half = channels // CORES
-    mine = lax.dynamic_slice_in_dim(term, core * half, half, 1)
-    other = lax.dynamic_slice_in_dim(term, (1 - core) * half, half, 1)
-    chip = mine.astype(jnp.float32) + lax.ppermute(other, "c", SWAP).astype(jnp.float32)
+
+    def term_of(start):
+        cols = lax.dynamic_slice_in_dim(out_grad, start, half, 2)
+        return sum(
+            lax.dot_general(
+                grn_out[i], cols[i], (((0,), (0,)), ((), ())), preferred_element_type=jnp.float32
+            )
+            for i in range(images)
+        ).astype(jnp.bfloat16)
+
+    sent = lax.ppermute(term_of((1 - core) * half), "c", SWAP)
+    chip = term_of(core * half).astype(jnp.float32) + sent.astype(jnp.float32)
     n_shard = lax.axis_size("shard")
     block = hidden // n_shard
     pieces = lax.all_to_all(

time: 166 us -> 158 us (0.952)
  local copies, waits for them, and re-layouts: 6.13 us -> 2.59 us
  other arithmetic: 8.51 us -> 6.25 us
    dynamic_slice x1 -> x0, local copies, waits for them, and re-layouts: 3.34 us -> none  [body(): other = lax.dynamic_slice_in_dim(term, (1 - core) * half, half, 1)]
    convert_element_type x1 -> x0, other arithmetic: 2.27 us -> none  [body(): chip.astype(jnp.bfloat16).reshape(n_shard, block, half)]
    dot_general x2 -> x4, matrix products: 5.17 us -> 4.42 us  [term_of(): lax.dot_general(grn_out[i], cols[i], (((0,), (0,)), ((), ())), preferred_...]
  transfers between devices with their start and end apart: 4 -> 4, of which waited for: 3 -> 3; matrix products, arithmetic and copies ran while one was open for 0% -> 1% of each run, Pallas kernels for 0% -> 0%
where the time goes in v7:
time: 158 us; the launch traced here: 155 us
  blocking collectives  123 us (78%)
  starting transfers between devices  9.49 us (6%)
  waiting for transfers between devices  8.76 us (6%)
  other arithmetic  6.25 us (4%)
  matrix products  4.42 us (3%)
  local copies, waits for them, and re-layouts  2.59 us (2%)
    all_to_all x1, blocking collectives, body(): lax.all_to_all(chip.astype(jnp.bfloat16).reshape(n_shard, block, half), '...  64.5 us
    all_to_all x1, blocking collectives, body(): lax.all_to_all(part.astype(jnp.bfloat16).reshape(n_xz, sub, half), ('xl',...  27.7 us
    all_to_all x1, blocking collectives, body(): lax.all_to_all(spread_cols, 'shard', 0, 0, tiled=True)  15.3 us
    all_to_all x1, blocking collectives, body(): lax.all_to_all(spread, 'z', 0, 0, tiled=True).reshape(rows_half, half)  15.1 us
    dot_general x4, matrix products, term_of(): lax.dot_general(grn_out[i], cols[i], (((0,), (0,)), ((), ())), preferred_...  4.42 us
    ppermute x1, starting transfers between devices, body(): from_x = lax.ppermute(grad_quarter, 'xl', SWAP)  3.45 us
    ppermute x1, waiting for transfers between devices, body(): sent = lax.ppermute(term_of((1 - core) * half), 'c', SWAP)  3.41 us
  transfers between devices with their start and end apart: 4, of which 3 were waited for; matrix products, arithmetic and copies ran while one was open for 1% of the time, Pallas kernels for 0%

profile of v7, /device:TPU:6, one launch (start us, length us, event | category | flops | bytes accessed | tf_op | source)
XLA Modules:
  0.0 155.0 jit_solution(10866736579867727507)
XLA Ops:
  0.6 0.0 copy-start
  0.6 0.0 copy-start.6
  0.7 0.0 copy-start.7
  0.7 2.5 %fusion = f32[2,3072]{1,0:T(2,128)S(1)} fusion(bf16[2,196,3072]{2,0,1:T(2,128)(2,1)} %param.7), kind=kLoop, calls=%fused_computation.3 | loop fusion | flops 3606528 | bytes 2433024 | tf_op jit(solution)/shard_map/reduce_sum | solution.py:20
  3.1 0.1 sqrt_reduce_fusion
  3.3 0.1 sqrt_divide_fusion
  3.4 0.0 copy-done
  3.4 0.0 copy-done.6
  3.4 0.0 copy-done.7
  3.4 0.0 copy-start.1
  3.4 1.0 fusion.3
  4.4 0.1 copy-done.1
  4.5 1.5 constant_dynamic-slice_fusion.3
  5.9 1.1 fusion.4
  7.0 1.1 add_convert_fusion.1
  8.1 1.9 %collective-permute-start = (bf16[3072,384]{1,0:T(8,128)(2,1)S(1)}, bf16[3072,384]{1,0:T(8,128)(2,1)S(1)}, u32[]{:S(2)}, u32[]{:S(2)}) collective-permute-start(bf16[3072,384]{1,0:T(8,128)(2,1)S(1)} %add_convert_fusion.1), channel_id=1, source_target_pairs={{0,1},{1,0},{2,3},{3,2},{4,5},{5,4},{6,7},{7,6},{8,9},{9,8},{10,11... | collective-permute-start | bytes 7077896 | tf_op jit(solution)/shard_map/ppermute | solution.py:46
  10.1 1.1 fusion.5
  11.2 3.4 %collective-permute-done = bf16[3072,384]{1,0:T(8,128)(2,1)S(1)} collective-permute-done((bf16[3072,384]{1,0:T(8,128)(2,1)S(1)}, bf16[3072,384]{1,0:T(8,128)(2,1)S(1)}, u32[]{:S(2)}, u32[]{:S(2)}) %collective-permute-start) | collective-permute-done | bytes 2359328 | tf_op jit(solution)/shard_map/ppermute | solution.py:46
  14.6 1.1 add_convert_fusion
  15.7 64.5 %all_to_all.20 = bf16[16,192,384]{2,1,0:T(8,128)(2,1)S(1)} all-to-all(bf16[16,192,384]{2,1,0:T(8,128)(2,1)S(1)} %bitcast.25), channel_id=1, replica_groups=mesh['shard'=16,'xl'=2,'z'=12,'c'=2] {'shard'}, dimensions={0} | all-to-all | bytes 4718592 | tf_op jit(solution)/shard_map/all_to_all | solution.py:50
  80.2 0.0 copy-start.3
  80.2 0.0 copy-start.4
  80.2 1.0 reduce_sum.41
  81.2 0.0 copy-start.5
  81.3 27.7 %all_to_all.21 = bf16[24,8,384]{2,1,0:T(8,128)(2,1)S(1)} all-to-all(bf16[24,8,384]{2,1,0:T(8,128)(2,1)} %bitcast.30), channel_id=1, replica_groups=mesh['shard'=16,'xl'=2,'z'=12,'c'=2] {'xl','z'}, dimensions={0} | all-to-all | bytes 294912 | tf_op jit(solution)/shard_map/all_to_all | solution.py:59
  109.0 15.1 %all_to_all.22 = f32[12,8,384]{2,1,0:T(8,128)S(1)} all-to-all(f32[12,8,384]{2,1,0:T(8,128)S(1)} %broadcast_in_dim.4), channel_id=1, replica_groups=mesh['shard'=16,'xl'=2,'z'=12,'c'=2] {'z'}, dimensions={0} | all-to-all | bytes 294912 | tf_op jit(solution)/shard_map/all_to_all | solution.py:64
  124.1 1.9 %collective-permute-start.1 = (f32[96,384]{1,0:T(8,128)S(1)}, f32[96,384]{1,0:T(8,128)S(1)}, u32[]{:S(2)}, u32[]{:S(2)}) collective-permute-start(f32[96,384]{1,0:T(8,128)S(1)} %bitcast.26), channel_id=1, source_target_pairs={{0,1},{1,0},{2,3},{3,2},{4,5},{5,4},{6,7},{7,6},{8,9},{9,8},{10,11... | collective-permute-start | bytes 442376 | tf_op jit(solution)/shard_map/ppermute | solution.py:66
  126.0 3.4 %collective-permute-start.2 = (f32[96,384]{1,0:T(8,128)S(1)}, f32[96,384]{1,0:T(8,128)S(1)}, u32[]{:S(2)}, u32[]{:S(2)}) collective-permute-start(f32[96,384]{1,0:T(8,128)S(1)} %bitcast.27), channel_id=1, source_target_pairs={{0,24},{24,0},{1,25},{25,1},{2,26},{26,2},{3,27},{27,3},{4,28},{28... | collective-permute-start | bytes 442376 | tf_op jit(solution)/shard_map/ppermute | solution.py:65
  129.5 2.2 %collective-permute-start.3 = (f32[96,384]{1,0:T(8,128)S(1)}, f32[96,384]{1,0:T(8,128)S(1)}, u32[]{:S(2)}, u32[]{:S(2)}) collective-permute-start(f32[96,384]{1,0:T(8,128)S(1)} %bitcast.28), channel_id=1, source_target_pairs={{0,25},{25,0},{1,24},{24,1},{2,27},{27,2},{3,26},{26,3},{4,29},{29... | collective-permute-start | bytes 442376 | tf_op jit(solution)/shard_map/ppermute | solution.py:67
  131.7 0.0 collective-permute-done.1
  131.8 2.4 %collective-permute-done.2 = f32[96,384]{1,0:T(8,128)S(1)} collective-permute-done((f32[96,384]{1,0:T(8,128)S(1)}, f32[96,384]{1,0:T(8,128)S(1)}, u32[]{:S(2)}, u32[]{:S(2)}) %collective-permute-start.2) | collective-permute-done | bytes 147488 | tf_op jit(solution)/shard_map/ppermute | solution.py:65
  134.1 3.0 %collective-permute-done.3 = f32[96,384]{1,0:T(8,128)S(1)} collective-permute-done((f32[96,384]{1,0:T(8,128)S(1)}, f32[96,384]{1,0:T(8,128)S(1)}, u32[]{:S(2)}, u32[]{:S(2)}) %collective-permute-start.3) | collective-permute-done | bytes 147488 | tf_op jit(solution)/shard_map/ppermute | solution.py:67
  137.1 0.0 copy-done.3
  137.1 0.0 copy-done.4
  137.1 0.0 copy-done.5
  137.2 1.5 multiply_subtract_fusion
  138.6 0.0 copy-start.2
  138.6 0.1 dynamic-slice_convert_fusion
  138.7 0.1 copy.28
  138.8 15.3 %all_to_all.23 = bf16[16,192,16]{1,2,0:T(8,128)(2,1)S(1)} all-to-all(bf16[16,192,16]{1,2,0:T(8,128)(2,1)S(1)} %broadcast_in_dim.5), channel_id=1, replica_groups=mesh['shard'=16,'xl'=2,'z'=12,'c'=2] {'shard'}, dimensions={0} | all-to-all | bytes 196608 | tf_op jit(solution)/shard_map/all_to_all | solution.py:82
  154.1 0.8 reshape.48
  155.0 0.0 copy-done.2
  (7 shorter events, 0.2 us)
Async XLA Ops:
  0.6 2.7 %copy-start = (bf16[2,196,3072]{2,0,1:T(2,128)(2,1)S(1)}, bf16[2,196,3072]{2,0,1:T(2,128)(2,1)}, u32[]{:S(2)}) copy-start(bf16[2,196,3072]{2,0,1:T(2,128)(2,1)} %param.7) | copy-start | bytes 7225348
  0.6 2.7 %copy-start.6 = (f32[3072]{0:T(1024)S(1)}, f32[3072]{0:T(1024)}, u32[]{:S(2)}) copy-start(f32[3072]{0:T(1024)} %param.10) | copy-start | bytes 36868
  0.7 2.7 %copy-start.7 = (f32[3072]{0:T(1024)S(1)}, f32[3072]{0:T(1024)}, u32[]{:S(2)}) copy-start(f32[3072]{0:T(1024)} %param.9) | copy-start | bytes 36868
  3.4 1.1 copy-start.1
  8.1 6.4 %collective-permute-start = (bf16[3072,384]{1,0:T(8,128)(2,1)S(1)}, bf16[3072,384]{1,0:T(8,128)(2,1)S(1)}, u32[]{:S(2)}, u32[]{:S(2)}) collective-permute-start(bf16[3072,384]{1,0:T(8,128)(2,1)S(1)} %add_convert_fusion.1), channel_id=1, source_target_pairs={{0,1},{1,0},{2,3},{3,2},{4,5},{5,4},{6,7},{7,6},{8,9},{9,8},{10,11... | collective-permute-start | bytes 7077896 | tf_op jit(solution)/shard_map/ppermute | solution.py:46
  80.2 56.9 %copy-start.3 = (f32[192,768]{1,0:T(8,128)S(1)}, f32[192,768]{1,0:T(8,128)}, u32[]{:S(2)}) copy-start(f32[192,768]{1,0:T(8,128)} %param.11) | copy-start | bytes 1769476
  80.2 56.9 %copy-start.4 = (f32[192,768]{1,0:T(8,128)S(1)}, f32[192,768]{1,0:T(8,128)}, u32[]{:S(2)}) copy-start(f32[192,768]{1,0:T(8,128)} %param.12) | copy-start | bytes 1769476
  81.2 55.9 %copy-start.5 = (f32[192,768]{1,0:T(8,128)S(1)}, f32[192,768]{1,0:T(8,128)}, u32[]{:S(2)}) copy-start(f32[192,768]{1,0:T(8,128)} %param.13) | copy-start | bytes 1769476
  124.1 7.6 %collective-permute-start.1 = (f32[96,384]{1,0:T(8,128)S(1)}, f32[96,384]{1,0:T(8,128)S(1)}, u32[]{:S(2)}, u32[]{:S(2)}) collective-permute-start(f32[96,384]{1,0:T(8,128)S(1)} %bitcast.26), channel_id=1, source_target_pairs={{0,1},{1,0},{2,3},{3,2},{4,5},{5,4},{6,7},{7,6},{8,9},{9,8},{10,11... | collective-permute-start | bytes 442376 | tf_op jit(solution)/shard_map/ppermute | solution.py:66
  126.0 8.1 %collective-permute-start.2 = (f32[96,384]{1,0:T(8,128)S(1)}, f32[96,384]{1,0:T(8,128)S(1)}, u32[]{:S(2)}, u32[]{:S(2)}) collective-permute-start(f32[96,384]{1,0:T(8,128)S(1)} %bitcast.27), channel_id=1, source_target_pairs={{0,24},{24,0},{1,25},{25,1},{2,26},{26,2},{3,27},{27,3},{4,28},{28... | collective-permute-start | bytes 442376 | tf_op jit(solution)/shard_map/ppermute | solution.py:65
  129.5 7.6 %collective-permute-start.3 = (f32[96,384]{1,0:T(8,128)S(1)}, f32[96,384]{1,0:T(8,128)S(1)}, u32[]{:S(2)}, u32[]{:S(2)}) collective-permute-start(f32[96,384]{1,0:T(8,128)S(1)} %bitcast.28), channel_id=1, source_target_pairs={{0,25},{25,0},{1,24},{24,1},{2,27},{27,2},{3,26},{26,3},{4,29},{29... | collective-permute-start | bytes 442376 | tf_op jit(solution)/shard_map/ppermute | solution.py:67
  138.6 16.3 %copy-start.2 = (f32[192,768]{1,0:T(8,128)}, f32[192,768]{1,0:T(8,128)S(1)}, u32[]{:S(2)}) copy-start(f32[192,768]{1,0:T(8,128)S(1)} %get-tuple-element.4) | copy-start | bytes 1769476

commit v8 on v7

--- a/solution.py
+++ b/solution.py
@@ -60,11 +60,12 @@
         part.astype(jnp.bfloat16).reshape(n_xz, sub, half), ("xl", "z"), 0, 0, tiled=True
     )
     grad_sub = jnp.sum(pieces2.astype(jnp.float32), axis=0)
-    spread = jnp.broadcast_to(grad_sub[None], (n_z, sub, half))
-    grad_quarter = lax.all_to_all(spread, "z", 0, 0, tiled=True).reshape(rows_half, half)
-    from_x = lax.ppermute(grad_quarter, "xl", SWAP)
-    from_core = lax.ppermute(grad_quarter, "c", SWAP)
-    from_both = lax.ppermute(grad_quarter, ("xl", "c"), [(0, 3), (3, 0), (1, 2), (2, 1)])
+    spread = jnp.broadcast_to(grad_sub.astype(jnp.bfloat16)[None], (n_z, sub, half))
+    sent_quarter = lax.all_to_all(spread, "z", 0, 0, tiled=True).reshape(rows_half, half)
+    grad_quarter = sent_quarter.astype(jnp.float32)
+    from_x = lax.ppermute(sent_quarter, "xl", SWAP).astype(jnp.float32)
+    from_core = lax.ppermute(sent_quarter, "c", SWAP).astype(jnp.float32)
+    from_both = lax.ppermute(sent_quarter, ("xl", "c"), [(0, 3), (3, 0), (1, 2), (2, 1)]).astype(jnp.float32)
     own_half = by_core(core, grad_quarter, from_core)
     far_half = by_core(core, from_x, from_both)
     grad = jnp.where(x_lo == 0, jnp.concatenate([own_half, far_half], 0), jnp.concatenate([far_half, own_half], 0))

time: 158 us -> 154 us (0.975)
  blocking collectives: 123 us -> 107 us
  waiting for transfers between devices: 8.76 us -> 15.7 us
  starting transfers between devices: 9.49 us -> 13.3 us
    all_to_all x1 -> x0, blocking collectives: 15.1 us -> none  [body(): lax.all_to_all(spread, 'z', 0, 0, tiled=True).reshape(rows_half, half)]
    all_to_all x0 -> x1, waiting for transfers between devices: none -> 11.1 us  [body(): lax.all_to_all(spread, 'z', 0, 0, tiled=True).reshape(rows_half, half)]
    ppermute x3, waiting for transfers between devices: 5.35 us -> 1.18 us  [the longest x1 1.17 us: body(): lax.ppermute(sent_quarter, ('xl', 'c'), [(0, 3), (3, 0), (1, 2), (2, 1)])]
    all_to_all x0 -> x1, starting transfers between devices: none -> 3.5 us  [body(): lax.all_to_all(spread, 'z', 0, 0, tiled=True).reshape(rows_half, half)]
  transfers between devices with their start and end apart: 4 -> 5, of which waited for: 3 -> 3; matrix products, arithmetic and copies ran while one was open for 1% -> 1% of each run, Pallas kernels for 0% -> 0%
where the time goes in v8:
time: 154 us; the launch traced here: 151 us
  blocking collectives  107 us (69%)
  waiting for transfers between devices  15.7 us (10%)
  starting transfers between devices  13.3 us (9%)
  other arithmetic  6.3 us (4%)
  matrix products  4.42 us (3%)
  local copies, waits for them, and re-layouts  3.22 us (2%)
    all_to_all x1, blocking collectives, body(): lax.all_to_all(chip.astype(jnp.bfloat16).reshape(n_shard, block, half), '...  64.5 us
    all_to_all x1, blocking collectives, body(): lax.all_to_all(part.astype(jnp.bfloat16).reshape(n_xz, sub, half), ('xl',...  27.7 us
    all_to_all x1, blocking collectives, body(): lax.all_to_all(spread_cols, 'shard', 0, 0, tiled=True)  15.1 us
    all_to_all x1, waiting for transfers between devices, body(): lax.all_to_all(spread, 'z', 0, 0, tiled=True).reshape(rows_half, half)  11.1 us
    dot_general x4, matrix products, term_of(): lax.dot_general(grn_out[i], cols[i], (((0,), (0,)), ((), ())), preferred_...  4.42 us
    all_to_all x1, starting transfers between devices, body(): lax.all_to_all(spread, 'z', 0, 0, tiled=True).reshape(rows_half, half)  3.5 us
    ppermute x1, starting transfers between devices, body(): from_x = lax.ppermute(sent_quarter, 'xl', SWAP).astype(jnp.float32)  3.42 us
    ppermute x1, waiting for transfers between devices, body(): sent = lax.ppermute(term_of((1 - core) * half), 'c', SWAP)  3.41 us
  transfers between devices with their start and end apart: 5, of which 3 were waited for; matrix products, arithmetic and copies ran while one was open for 1% of the time, Pallas kernels for 0%

profile of v8, /device:TPU:6, one launch (start us, length us, event | category | flops | bytes accessed | tf_op | source)
XLA Modules:
  0.0 151.1 jit_solution(5570430643419673095)
XLA Ops:
  0.6 0.0 copy-start
  0.6 0.0 copy-start.6
  0.7 0.0 copy-start.7
  0.7 2.5 %fusion = f32[2,3072]{1,0:T(2,128)S(1)} fusion(bf16[2,196,3072]{2,0,1:T(2,128)(2,1)} %param.7), kind=kLoop, calls=%fused_computation.3 | loop fusion | flops 3606528 | bytes 2433024 | tf_op jit(solution)/shard_map/reduce_sum | solution.py:20
  3.1 0.1 sqrt_reduce_fusion
  3.3 0.1 sqrt_divide_fusion
  3.4 0.0 copy-done
  3.4 0.0 copy-done.6
  3.4 0.0 copy-done.7
  3.4 0.0 copy-start.1
  3.4 1.0 fusion.3
  4.4 0.1 copy-done.1
  4.5 1.5 constant_dynamic-slice_fusion.3
  5.9 1.1 fusion.4
  7.0 1.1 add_convert_fusion.1
  8.1 1.9 %collective-permute-start = (bf16[3072,384]{1,0:T(8,128)(2,1)S(1)}, bf16[3072,384]{1,0:T(8,128)(2,1)S(1)}, u32[]{:S(2)}, u32[]{:S(2)}) collective-permute-start(bf16[3072,384]{1,0:T(8,128)(2,1)S(1)} %add_convert_fusion.1), channel_id=1, source_target_pairs={{0,1},{1,0},{2,3},{3,2},{4,5},{5,4},{6,7},{7,6},{8,9},{9,8},{10,11... | collective-permute-start | bytes 7077896 | tf_op jit(solution)/shard_map/ppermute | solution.py:46
  10.1 1.1 fusion.5
  11.2 3.4 %collective-permute-done = bf16[3072,384]{1,0:T(8,128)(2,1)S(1)} collective-permute-done((bf16[3072,384]{1,0:T(8,128)(2,1)S(1)}, bf16[3072,384]{1,0:T(8,128)(2,1)S(1)}, u32[]{:S(2)}, u32[]{:S(2)}) %collective-permute-start) | collective-permute-done | bytes 2359328 | tf_op jit(solution)/shard_map/ppermute | solution.py:46
  14.6 1.1 add_convert_fusion
  15.7 64.5 %all_to_all.20 = bf16[16,192,384]{2,1,0:T(8,128)(2,1)S(1)} all-to-all(bf16[16,192,384]{2,1,0:T(8,128)(2,1)S(1)} %bitcast.26), channel_id=1, replica_groups=mesh['shard'=16,'xl'=2,'z'=12,'c'=2] {'shard'}, dimensions={0} | all-to-all | bytes 4718592 | tf_op jit(solution)/shard_map/all_to_all | solution.py:50
  80.2 0.0 copy-start.3
  80.2 0.0 copy-start.4
  80.2 1.0 reduce_sum.44
  81.2 0.0 copy-start.5
  81.3 27.7 %all_to_all.21 = bf16[24,8,384]{2,1,0:T(8,128)(2,1)S(1)} all-to-all(bf16[24,8,384]{2,1,0:T(8,128)(2,1)} %bitcast.27), channel_id=1, replica_groups=mesh['shard'=16,'xl'=2,'z'=12,'c'=2] {'xl','z'}, dimensions={0} | all-to-all | bytes 294912 | tf_op jit(solution)/shard_map/all_to_all | solution.py:59
  109.0 0.6 broadcast_in_dim.4
  109.6 3.5 %all-to-all-start.2 = ((bf16[12,8,384]{2,1,0:T(8,128)(2,1)}), bf16[12,8,384]{2,1,0:T(8,128)(2,1)S(1)}, u32[]{:S(2)}, u32[]{:S(2)}) async-start(bf16[12,8,384]{2,1,0:T(8,128)(2,1)} %broadcast_in_dim.4), calls=%async_computation.2 | async-start | bytes 147456 | tf_op jit(solution)/shard_map/all_to_all | solution.py:64
  113.2 11.1 %all-to-all-done.2 = bf16[12,8,384]{2,1,0:T(8,128)(2,1)S(1)} async-done(((bf16[12,8,384]{2,1,0:T(8,128)(2,1)}), bf16[12,8,384]{2,1,0:T(8,128)(2,1)S(1)}, u32[]{:S(2)}, u32[]{:S(2)}) %all-to-all-start.2) | async-done | bytes 73760 | tf_op jit(solution)/shard_map/all_to_all | solution.py:64
  124.3 3.4 %collective-permute-start.2 = (bf16[96,384]{1,0:T(8,128)(2,1)S(1)}, bf16[96,384]{1,0:T(8,128)(2,1)S(1)}, u32[]{:S(2)}, u32[]{:S(2)}) collective-permute-start(bf16[96,384]{1,0:T(8,128)(2,1)S(1)} %bitcast.28), channel_id=1, source_target_pairs={{0,24},{24,0},{1,25},{25,1},{2,26},{26,2},{3,27},{27,3},{4,28},{28... | collective-permute-start | bytes 221192 | tf_op jit(solution)/shard_map/ppermute | solution.py:66
  127.7 1.9 %collective-permute-start.3 = (bf16[96,384]{1,0:T(8,128)(2,1)S(1)}, bf16[96,384]{1,0:T(8,128)(2,1)S(1)}, u32[]{:S(2)}, u32[]{:S(2)}) collective-permute-start(bf16[96,384]{1,0:T(8,128)(2,1)S(1)} %bitcast.29), channel_id=1, source_target_pairs={{0,25},{25,0},{1,24},{24,1},{2,27},{27,2},{3,26},{26,3},{4,29},{29... | collective-permute-start | bytes 221192 | tf_op jit(solution)/shard_map/ppermute | solution.py:68
  129.6 2.5 %collective-permute-start.1 = (bf16[96,384]{1,0:T(8,128)(2,1)S(1)}, bf16[96,384]{1,0:T(8,128)(2,1)S(1)}, u32[]{:S(2)}, u32[]{:S(2)}) collective-permute-start(bf16[96,384]{1,0:T(8,128)(2,1)S(1)} %bitcast.30), channel_id=1, source_target_pairs={{0,1},{1,0},{2,3},{3,2},{4,5},{5,4},{6,7},{7,6},{8,9},{9,8},{10,11... | collective-permute-start | bytes 221192 | tf_op jit(solution)/shard_map/ppermute | solution.py:67
  132.2 0.0 collective-permute-done.2
  132.2 1.2 collective-permute-done.3
  133.4 0.0 collective-permute-done.1
  133.5 0.0 copy-done.3
  133.5 0.0 copy-done.4
  133.5 0.0 copy-done.5
  133.5 1.5 multiply_subtract_fusion
  135.0 0.0 copy-start.2
  135.0 0.1 dynamic-slice_convert_fusion
  135.1 0.1 copy.28
  135.2 15.1 %all_to_all.22 = bf16[16,192,16]{1,2,0:T(8,128)(2,1)S(1)} all-to-all(bf16[16,192,16]{1,2,0:T(8,128)(2,1)S(1)} %broadcast_in_dim.5), channel_id=1, replica_groups=mesh['shard'=16,'xl'=2,'z'=12,'c'=2] {'shard'}, dimensions={0} | all-to-all | bytes 196608 | tf_op jit(solution)/shard_map/all_to_all | solution.py:83
  150.3 0.8 reshape.48
  151.1 0.0 copy-done.2
  (10 shorter events, 0.2 us)
Async XLA Ops:
  0.6 2.7 %copy-start = (bf16[2,196,3072]{2,0,1:T(2,128)(2,1)S(1)}, bf16[2,196,3072]{2,0,1:T(2,128)(2,1)}, u32[]{:S(2)}) copy-start(bf16[2,196,3072]{2,0,1:T(2,128)(2,1)} %param.7) | copy-start | bytes 7225348
  0.6 2.7 %copy-start.6 = (f32[3072]{0:T(1024)S(1)}, f32[3072]{0:T(1024)}, u32[]{:S(2)}) copy-start(f32[3072]{0:T(1024)} %param.10) | copy-start | bytes 36868
  0.7 2.7 %copy-start.7 = (f32[3072]{0:T(1024)S(1)}, f32[3072]{0:T(1024)}, u32[]{:S(2)}) copy-start(f32[3072]{0:T(1024)} %param.9) | copy-start | bytes 36868
  3.4 1.1 copy-start.1
  8.1 6.4 %collective-permute-start = (bf16[3072,384]{1,0:T(8,128)(2,1)S(1)}, bf16[3072,384]{1,0:T(8,128)(2,1)S(1)}, u32[]{:S(2)}, u32[]{:S(2)}) collective-permute-start(bf16[3072,384]{1,0:T(8,128)(2,1)S(1)} %add_convert_fusion.1), channel_id=1, source_target_pairs={{0,1},{1,0},{2,3},{3,2},{4,5},{5,4},{6,7},{7,6},{8,9},{9,8},{10,11... | collective-permute-start | bytes 7077896 | tf_op jit(solution)/shard_map/ppermute | solution.py:46
  80.2 53.2 %copy-start.3 = (f32[192,768]{1,0:T(8,128)S(1)}, f32[192,768]{1,0:T(8,128)}, u32[]{:S(2)}) copy-start(f32[192,768]{1,0:T(8,128)} %param.11) | copy-start | bytes 1769476
  80.2 53.3 %copy-start.4 = (f32[192,768]{1,0:T(8,128)S(1)}, f32[192,768]{1,0:T(8,128)}, u32[]{:S(2)}) copy-start(f32[192,768]{1,0:T(8,128)} %param.12) | copy-start | bytes 1769476
  81.2 52.3 %copy-start.5 = (f32[192,768]{1,0:T(8,128)S(1)}, f32[192,768]{1,0:T(8,128)}, u32[]{:S(2)}) copy-start(f32[192,768]{1,0:T(8,128)} %param.13) | copy-start | bytes 1769476
  109.6 14.6 %all-to-all-start.2 = ((bf16[12,8,384]{2,1,0:T(8,128)(2,1)}), bf16[12,8,384]{2,1,0:T(8,128)(2,1)S(1)}, u32[]{:S(2)}, u32[]{:S(2)}) async-start(bf16[12,8,384]{2,1,0:T(8,128)(2,1)} %broadcast_in_dim.4), calls=%async_computation.2 | async-start | bytes 147456 | tf_op jit(solution)/shard_map/all_to_all | solution.py:64
  124.3 7.9 %collective-permute-start.2 = (bf16[96,384]{1,0:T(8,128)(2,1)S(1)}, bf16[96,384]{1,0:T(8,128)(2,1)S(1)}, u32[]{:S(2)}, u32[]{:S(2)}) collective-permute-start(bf16[96,384]{1,0:T(8,128)(2,1)S(1)} %bitcast.28), channel_id=1, source_target_pairs={{0,24},{24,0},{1,25},{25,1},{2,26},{26,2},{3,27},{27,3},{4,28},{28... | collective-permute-start | bytes 221192 | tf_op jit(solution)/shard_map/ppermute | solution.py:66
  127.7 5.7 %collective-permute-start.3 = (bf16[96,384]{1,0:T(8,128)(2,1)S(1)}, bf16[96,384]{1,0:T(8,128)(2,1)S(1)}, u32[]{:S(2)}, u32[]{:S(2)}) collective-permute-start(bf16[96,384]{1,0:T(8,128)(2,1)S(1)} %bitcast.29), channel_id=1, source_target_pairs={{0,25},{25,0},{1,24},{24,1},{2,27},{27,2},{3,26},{26,3},{4,29},{29... | collective-permute-start | bytes 221192 | tf_op jit(solution)/shard_map/ppermute | solution.py:68
  129.6 3.8 %collective-permute-start.1 = (bf16[96,384]{1,0:T(8,128)(2,1)S(1)}, bf16[96,384]{1,0:T(8,128)(2,1)S(1)}, u32[]{:S(2)}, u32[]{:S(2)}) collective-permute-start(bf16[96,384]{1,0:T(8,128)(2,1)S(1)} %bitcast.30), channel_id=1, source_target_pairs={{0,1},{1,0},{2,3},{3,2},{4,5},{5,4},{6,7},{7,6},{8,9},{9,8},{10,11... | collective-permute-start | bytes 221192 | tf_op jit(solution)/shard_map/ppermute | solution.py:67
  135.0 16.1 %copy-start.2 = (f32[192,768]{1,0:T(8,128)}, f32[192,768]{1,0:T(8,128)S(1)}, u32[]{:S(2)}) copy-start(f32[192,768]{1,0:T(8,128)S(1)} %get-tuple-element.4) | copy-start | bytes 1769476
